TPU v7x, 128 devices: a whole 4x4x4 slice. The times are simulated.
128 devices in a mesh: seq: 32 (over y, z, core), tp: 4 (over x).
Axes of the slice: x: 4, y: 4, z: 4, core: 2. Of those that a mesh axis runs over, the one named last changes fastest.
Arguments:
- residual: bfloat16 [8192, 3584], P(('seq', 'tp')), may hold values from -6 to 6
- x_in: bfloat16 [8192, 3584], P('seq', 'tp'), may hold values from -6 to 6
- z_in: bfloat16 [8192, 3584], P('seq', 'tp'), may hold values from -6 to 6
- bc_in: bfloat16 [8192, 128], P('seq'), may hold values from -1.5 to 1.5
- dt_in: float32 [8192, 56], P('seq', 'tp'), may hold values from -6 to 6
- conv_x_weight: float32 [4, 3584], P(None, 'tp'), may hold values from -3 to 3
- conv_bc_weight: float32 [4, 128], replicated, may hold values from -3 to 3
- conv_x_cache: bfloat16 [16, 3, 3584], P(None, None, 'tp'), may hold values from -6 to 6
- conv_bc_cache: bfloat16 [16, 3, 128], replicated, may hold values from -1.5 to 1.5
- ssm_cache: float32 [16, 56, 64, 64], P(None, 'tp'), may hold values from -12 to 12
- dt_bias: float32 [56], P('tp'), may hold values from -1 to 1
- a_log: float32 [56], P('tp'), may hold values from -9 to -3.5
- d_skip: float32 [56], P('tp'), may hold values from 0.5 to 1.5
- norm_gain: float32 [3584], P('tp'), may hold values from 0.5 to 1.5
- out_weight: bfloat16 [3584, 3584], P('tp'), may hold values from -0.09375 to 0.09375
- attn_gain: float32 [3584], replicated, may hold values from 0.5 to 1.5
- q_weight: bfloat16 [3584, 3584], P(None, 'tp'), may hold values from -1 to 1
- q_down: bfloat16 [3584, 128], replicated, may hold values from -0.09375 to 0.09375
- q_up: bfloat16 [128, 3584], P(None, 'tp'), may hold values from -0.5 to 0.5
- cache_keys: bfloat16 [8192, 3584], P('seq', 'tp'), may hold values from -6 to 6
- cache_values: bfloat16 [8192, 3584], P('seq', 'tp'), may hold values from -6 to 6
- new_keys: bfloat16 [8192, 3584], P('seq', 'tp'), may hold values from -6 to 6
- new_values: bfloat16 [8192, 3584], P('seq', 'tp'), may hold values from -6 to 6
- lengths: int32 [16], replicated, may hold values from 1 to 2304, 8192 in all
Outputs:
- hidden: bfloat16 [8192, 3584], P(('seq', 'tp'))
- attended: bfloat16 [8192, 3584], P('seq', 'tp')
Inputs may be any that keep to these rules, and one draw needn't show every extreme that they name: lengths of the prompts' second halves sum to 8192; the largest is 2304.
All inputs are finite; a program needn't handle non-finite values.
Results may differ from a plain program's by a relative error of at most 0.014.
Values may be sent and summed in bfloat16 or wider, within the bound.
No kernel may reach another device: no remote copies, remote signals or barrier semaphores. Data moves between devices by JAX's collectives and lax.ppermute only.
A program may use at most 192 MiB of HBM per device.

v0:
```python
import jax
import jax.numpy as jnp
from jax import lax
from jax.sharding import PartitionSpec as P

HA = 224


EPS = 1e-05
NEG = -1e30


def shifted_2(value, axis, steps):
    count = lax.axis_size(axis)
    initial, last = (max(0, -steps), min(count, count - steps))
    return lax.ppermute(value, axis, [(source, source + steps) for source in range(initial, last)])


def locate(lengths, index):
    ends = jnp.cumsum(lengths)
    starts = ends - lengths
    count = lengths.shape[0]
    segment = jnp.sum((index[:, None] >= ends[None, :]).astype(jnp.int32), axis=1)
    segment = jnp.minimum(segment, count - 1)
    onehot = segment[:, None] == jnp.arange(count, dtype=jnp.int32)[None, :]
    begin = jnp.sum(jnp.where(onehot, starts[None, :], 0), axis=1)
    valid = (index >= 0) & (index < ends[count - 1])
    return (segment, begin, valid, onehot)


def convolve(inputs, border, cache, weight, position, onehot):
    taps = weight.shape[0]
    length = inputs.shape[0]
    extended = jnp.concatenate([border, inputs], axis=0)
    picks = onehot.astype(jnp.bfloat16)
    cached_rows = [
        jnp.dot(picks, cache[:, slot, :], preferred_element_type=jnp.float32)
        for slot in range(taps - 1)
    ]
    result = weight[0][None, :] * inputs.astype(jnp.float32)
    for lag in range(1, taps):
        shifted = extended[taps - 1 - lag : taps - 1 - lag + length].astype(jnp.float32)
        slot_index = taps - 1 + position - lag
        fallback = jnp.zeros_like(shifted)
        for slot in range(taps - 1):
            fallback = jnp.where((slot_index == slot)[:, None], cached_rows[slot], fallback)
        shifted = jnp.where((position >= lag)[:, None], shifted, fallback)
        result = result + weight[lag][None, :] * shifted
    return jax.nn.silu(result).astype(jnp.bfloat16)


def per_device(
    residual,
    x_in,
    z_in,
    bc_in,
    dt_in,
    conv_x_weight,
    conv_bc_weight,
    conv_x_cache,
    conv_bc_cache,
    ssm_cache,
    dt_bias,
    a_log,
    d_skip,
    norm_gain,
    out_weight,
    attn_gain,
    q_weight,
    q_down,
    q_up,
    cache_keys,
    cache_values,
    new_keys,
    new_values,
    lengths,
):
    high_precision = lax.Precision.HIGH
    length = x_in.shape[0]
    taps = conv_x_weight.shape[0]
    seq_index = lax.axis_index("seq")
    seq_count = lax.axis_size("seq")
    reach = seq_count // 4 + 1
    first = seq_index * length
    long_hop = reach + 1
    tied_steps = 5
    behind_pieces = [jnp.stack([cache_keys, cache_values, new_keys, new_values])] * (reach + 1)
    forward_pieces = [jnp.stack([cache_keys, cache_values])] * (reach + 1)
    relay_steps = []
    for distance in range(1, long_hop):
        relay_steps.append([(distance, distance - 1, 1)])
    for distance in range(long_hop, reach + 1):
        relay_steps[distance - long_hop].append((distance, distance - long_hop, long_hop))

    def advance(values, tied=True):
        if not relay_steps or (tied and len(relay_steps) <= reach - tied_steps):
            return values
        moves = relay_steps.pop(0)
        sent = []
        for distance, source, steps in moves:
            sent.append(
                (
                    shifted_2(behind_pieces[source], "seq", steps),
                    shifted_2(forward_pieces[source], "seq", -steps),
                )
            )
        sent, values = lax.optimization_barrier((sent, values))
        for (distance, _, _), (behind, forward) in zip(moves, sent):
            behind_pieces[distance] = behind
            forward_pieces[distance] = forward
        return values

    local_index = first + jnp.arange(length, dtype=jnp.int32)
    segment, begin, valid, onehot = locate(lengths, local_index)
    position = local_index - begin
    x_border, bc_border = shifted_2(
        (x_in[length - taps + 1 :], bc_in[length - taps + 1 :]), "seq", 1
    )
    x_conv = convolve(x_in, x_border, conv_x_cache, conv_x_weight, position, onehot)
    bc_conv = convolve(bc_in, bc_border, conv_bc_cache, conv_bc_weight, position, onehot)
    x_conv, bc_conv = advance((x_conv, bc_conv))
    heads = dt_bias.shape[0]
    state_size = bc_in.shape[1] // 2
    head_size = x_in.shape[1] // heads
    prompts = lengths.shape[0]
    values_bf = x_conv.reshape(length, heads, head_size)
    values = x_conv.astype(jnp.float32).reshape(length, heads, head_size)
    inputs_b = bc_conv[:, :state_size]
    inputs_c = bc_conv[:, state_size:]
    step = jax.nn.softplus(dt_in + dt_bias[None, :])
    log_decay = -step * jnp.exp(a_log)[None, :]
    cumulative = jnp.cumsum(log_decay, axis=0)
    local_begin = jnp.maximum(begin - first, 0)
    before = jnp.take(cumulative - log_decay, local_begin, axis=0)
    from_begin = jnp.exp(cumulative - before)
    block = min(length, 512)
    pair_scores = jnp.dot(inputs_c, inputs_b.T, preferred_element_type=jnp.float32)
    cumulative_t = cumulative.T
    step_t = step.T
    order = jnp.arange(length, dtype=jnp.int32)

    def intra(block_start):
        query_rows = block_start + jnp.arange(block, dtype=jnp.int32)
        same = (segment[:, None] == segment[None, :]) & (query_rows[:, None] >= order[None, :])
        gap = cumulative_t[:, :, None] - cumulative_t[:, None, :]
        factor = jnp.where(same[None], jnp.exp(jnp.where(same[None], gap, 0.0)), 0.0)
        weights = factor * step_t[:, None, :] * pair_scores[None, :, :]
        return jnp.einsum(
            "hqs,shd->qhd",
            weights,
            values_bf,
            precision=high_precision,
            preferred_element_type=jnp.float32,
        )

    intra_out = lax.map(intra, jnp.arange(length // block, dtype=jnp.int32) * block).reshape(
        length, heads, head_size
    )
    last_segment = segment[length - 1]
    in_last = segment == last_segment
    tail_weight = (
        jnp.where(in_last[:, None], jnp.exp(cumulative[length - 1][None, :] - cumulative), 0.0)
        * step
    )
    weighted = tail_weight[:, :, None] * values
    local_state = jnp.einsum(
        "thd,tn->hdn",
        weighted,
        inputs_b,
        precision=high_precision,
        preferred_element_type=jnp.float32,
    )
    whole_decay = jnp.exp(cumulative[length - 1] - before[length - 1])
    starts_here = begin[length - 1] >= first
    cached_last = lax.dynamic_index_in_dim(ssm_cache, last_segment, 0, keepdims=False)
    chain_state = local_state + jnp.where(
        starts_here, whole_decay[:, None, None] * cached_last, 0.0
    )
    chain_decay = jnp.where(starts_here, jnp.zeros_like(whole_decay), whole_decay)

    scan_decay, scan_state = advance((chain_decay, chain_state))
    distance = 1
    while distance <= reach and distance < seq_count:
        prior_decay, prior_state = shifted_2((scan_decay, scan_state), "seq", distance)
        scan_state = scan_decay[:, None, None] * prior_state + scan_state
        scan_decay = scan_decay * prior_decay
        scan_decay, scan_state = advance((scan_decay, scan_state))
        distance *= 2
    carried = advance(shifted_2(scan_state, "seq", 1))
    continuing = position[0] > 0
    replace = (jnp.arange(prompts, dtype=jnp.int32) == segment[0]) & continuing
    initial = jnp.where(replace[:, None, None, None], carried[None], ssm_cache)
    selected = (onehot[:, :, None].astype(jnp.bfloat16) * inputs_c[:, None, :]).reshape(
        length, prompts * state_size
    )
    table = jnp.transpose(initial, (0, 3, 1, 2)).reshape(prompts * state_size, heads * head_size)
    init_out = (
        jnp.dot(
            selected, table, precision=high_precision, preferred_element_type=jnp.float32
        ).reshape(length, heads, head_size)
        * from_begin[:, :, None]
    )
    mixed = intra_out + init_out + d_skip[None, :, None] * values
    gated = (
        mixed * jax.nn.silu(z_in.astype(jnp.float32).reshape(length, heads, head_size))
    ).reshape(length, heads * head_size)
    gated = advance(gated)
    squares = lax.psum(jnp.sum(gated * gated, axis=1), "tp")
    width = gated.shape[1] * lax.axis_size("tp")
    normed = (gated * lax.rsqrt(squares / width + EPS)[:, None] * norm_gain[None, :]).astype(
        jnp.bfloat16
    )
    normed = advance(normed)
    summed = lax.psum_scatter(
        jnp.dot(normed, out_weight, preferred_element_type=jnp.float32),
        "tp",
        scatter_dimension=0,
        tiled=True,
    )
    hidden = (residual.astype(jnp.float32) + summed).astype(jnp.bfloat16)
    level = hidden.astype(jnp.float32)
    attn_in = (
        level * lax.rsqrt(jnp.mean(level * level, axis=1, keepdims=True) + EPS) * attn_gain[None, :]
    ).astype(jnp.bfloat16)
    piece = lax.all_gather(attn_in, "tp", axis=0, tiled=True)
    low = jnp.dot(piece, q_down, preferred_element_type=jnp.float32).astype(jnp.bfloat16)
    query = (
        jnp.dot(piece, q_weight, preferred_element_type=jnp.float32)
        + jnp.dot(low, q_up, preferred_element_type=jnp.float32)
    ).astype(jnp.bfloat16)
    count_heads = query.shape[1] // HA

    def piece_mask(query_index, query_segment, offset, causal):
        key_index = (seq_index + offset) * length + jnp.arange(length, dtype=jnp.int32)
        key_segment, _, key_valid, _ = locate(lengths, key_index)
        allowed = key_valid[None, :] & (key_segment[None, :] == query_segment[:, None])
        if causal:
            allowed = allowed & (key_index[None, :] <= query_index[:, None])
        return allowed

    cache_pieces = [(cache_keys, cache_values, 0)]
    new_pieces = [(new_keys, new_values, 0)]
    while relay_steps:
        advance((), tied=False)
    for distance in range(1, reach + 1):
        behind = behind_pieces[distance]
        cache_pieces.append((behind[0], behind[1], -distance))
        new_pieces.append((behind[2], behind[3], -distance))
        forward = forward_pieces[distance]
        cache_pieces.append((forward[0], forward[1], distance))
    all_keys = jnp.concatenate(
        [entry[0] for entry in cache_pieces] + [entry[0] for entry in new_pieces], axis=0
    )
    all_values = jnp.concatenate(
        [entry[1] for entry in cache_pieces] + [entry[1] for entry in new_pieces], axis=0
    )
    mask = jnp.concatenate(
        [piece_mask(local_index, segment, entry[2], False) for entry in cache_pieces]
        + [piece_mask(local_index, segment, entry[2], True) for entry in new_pieces],
        axis=1,
    )
    scale = 1.0 / HA**0.5

    def attend(head):
        column = head * HA
        query_head = lax.dynamic_slice_in_dim(query, column, HA, 1)
        key_head = lax.dynamic_slice_in_dim(all_keys, column, HA, 1)
        value_head = lax.dynamic_slice_in_dim(all_values, column, HA, 1)
        scores = (
            lax.dot_general(
                query_head, key_head, (((1,), (1,)), ((), ())), preferred_element_type=jnp.float32
            )
            * scale
        )
        scores = jnp.where(mask, scores, NEG)
        top = jnp.max(scores, axis=1, keepdims=True)
        weights = jnp.exp(scores - top)
        probs = (weights / jnp.sum(weights, axis=1, keepdims=True)).astype(jnp.bfloat16)
        return jnp.dot(probs, value_head, preferred_element_type=jnp.float32).astype(jnp.bfloat16)

    per_head = lax.map(attend, jnp.arange(count_heads, dtype=jnp.int32))
    attended = jnp.transpose(per_head, (1, 0, 2)).reshape(length, count_heads * HA)
    return (hidden, attended)


def solution(mesh):
    in_specs = (
        P(("seq", "tp"), None),
        P("seq", "tp"),
        P("seq", "tp"),
        P("seq", None),
        P("seq", "tp"),
        P(None, "tp"),
        P(),
        P(None, None, "tp"),
        P(),
        P(None, "tp", None, None),
        P("tp"),
        P("tp"),
        P("tp"),
        P("tp"),
        P("tp", None),
        P(),
        P(None, "tp"),
        P(),
        P(None, "tp"),
        P("seq", "tp"),
        P("seq", "tp"),
        P("seq", "tp"),
        P("seq", "tp"),
        P(),
    )
    out_specs = (P(("seq", "tp"), None), P("seq", "tp"))
    return jax.shard_map(
        per_device, mesh=mesh, in_specs=in_specs, out_specs=out_specs, check_vma=False
    )
```

profile of v0, /device:TPU:16, one launch (start us, length us, event | category | flops | bytes accessed | tf_op | source)
XLA Modules:
  0.0 464.1 jit_solution(2392383028275944410)
XLA Ops:
  14.4 5.7 %collective-permute-start.1 = (bf16[2,256,896]{2,1,0:T(8,128)(2,1)}, bf16[2,256,896]{2,1,0:T(8,128)(2,1)}, u32[]{:S(2)}, u32[]{:S(2)}) collective-permute-start(bf16[2,256,896]{2,1,0:T(8,128)(2,1)} %pad_maximum_fusion.1), channel_id=1, source_target_pairs={{4,0},{8,4},{12,8},{16,12},{20,16},{24,20},{28,24},{32,28},{36,32}... | collective-permute-start | bytes 2752520 | tf_op jit(solution)/shard_map/ppermute | solution.py:16
  57.4 5.6 %collective-permute-start.5 = (bf16[2,256,896]{2,1,0:T(8,128)(2,1)}, bf16[2,256,896]{2,1,0:T(8,128)(2,1)}, u32[]{:S(2)}, u32[]{:S(2)}) collective-permute-start(bf16[2,256,896]{2,1,0:T(8,128)(2,1)} %collective-permute-done.1), channel_id=1, source_target_pairs={{4,0},{8,4},{12,8},{16,12},{20,16},{24,20},{28,24},{32,28},{36,32}... | collective-permute-start | bytes 2752520 | tf_op jit(solution)/shard_map/ppermute | solution.py:16
  66.5 7.7 %collective-permute-done.5 = bf16[2,256,896]{2,1,0:T(8,128)(2,1)} collective-permute-done((bf16[2,256,896]{2,1,0:T(8,128)(2,1)}, bf16[2,256,896]{2,1,0:T(8,128)(2,1)}, u32[]{:S(2)}, u32[]{:S(2)}) %collective-permute-start.5) | collective-permute-done | bytes 917536 | tf_op jit(solution)/shard_map/ppermute | solution.py:16
  80.9 5.8 %collective-permute-start.7 = (bf16[2,256,896]{2,1,0:T(8,128)(2,1)}, bf16[2,256,896]{2,1,0:T(8,128)(2,1)}, u32[]{:S(2)}, u32[]{:S(2)}) collective-permute-start(bf16[2,256,896]{2,1,0:T(8,128)(2,1)} %collective-permute-done.5), channel_id=1, source_target_pairs={{4,0},{8,4},{12,8},{16,12},{20,16},{24,20},{28,24},{32,28},{36,32}... | collective-permute-start | bytes 2752520 | tf_op jit(solution)/shard_map/ppermute | solution.py:16
  91.4 17.6 %collective-permute-done.8 = f32[14]{0:T(128)S(1)} collective-permute-done((f32[14]{0:T(128)S(1)}, f32[14]{0:T(128)S(1)}, u32[]{:S(2)}, u32[]{:S(2)}) %collective-permute-start.8) | collective-permute-done | bytes 88 | tf_op jit(solution)/shard_map/ppermute | solution.py:16
  112.5 5.8 %collective-permute-start.11 = (bf16[2,256,896]{2,1,0:T(8,128)(2,1)}, bf16[2,256,896]{2,1,0:T(8,128)(2,1)}, u32[]{:S(2)}, u32[]{:S(2)}) collective-permute-start(bf16[2,256,896]{2,1,0:T(8,128)(2,1)} %collective-permute-done.7), channel_id=1, source_target_pairs={{4,0},{8,4},{12,8},{16,12},{20,16},{24,20},{28,24},{32,28},{36,32}... | collective-permute-start | bytes 2752520 | tf_op jit(solution)/shard_map/ppermute | solution.py:16
  126.7 10.9 %collective-permute-done.12 = f32[14]{0:T(128)S(1)} collective-permute-done((f32[14]{0:T(128)S(1)}, f32[14]{0:T(128)S(1)}, u32[]{:S(2)}, u32[]{:S(2)}) %collective-permute-start.12) | collective-permute-done | bytes 88 | tf_op jit(solution)/shard_map/ppermute | solution.py:16
  141.8 8.7 %collective-permute-start.14 = (bf16[4,256,896]{2,1,0:T(8,128)(2,1)}, bf16[4,256,896]{2,1,0:T(8,128)(2,1)}, u32[]{:S(2)}, u32[]{:S(2)}) collective-permute-start(bf16[4,256,896]{2,1,0:T(8,128)(2,1)} %collective-permute-done.10), channel_id=1, source_target_pairs={{0,4},{4,8},{8,12},{12,16},{16,20},{20,24},{24,28},{28,32},{32,36}... | collective-permute-start | bytes 5505032 | tf_op jit(solution)/shard_map/ppermute | solution.py:16
  156.4 6.1 %collective-permute-start.16 = (f32[14]{0:T(128)S(1)}, f32[14]{0:T(128)S(1)}, u32[]{:S(2)}, u32[]{:S(2)}) collective-permute-start(f32[14]{0:T(128)S(1)} %mul.387), channel_id=1, source_target_pairs={{0,16},{4,20},{8,24},{12,28},{16,32},{20,36},{24,40},{28,44},{32,4... | collective-permute-start | bytes 176 | tf_op jit(solution)/shard_map/ppermute | solution.py:16
  162.6 16.6 %collective-permute-done.16 = f32[14]{0:T(128)S(1)} collective-permute-done((f32[14]{0:T(128)S(1)}, f32[14]{0:T(128)S(1)}, u32[]{:S(2)}, u32[]{:S(2)}) %collective-permute-start.16) | collective-permute-done | bytes 88 | tf_op jit(solution)/shard_map/ppermute | solution.py:16
  188.2 7.9 %collective-permute-done.18 = f32[14,64,64]{2,1,0:T(8,128)S(1)} collective-permute-done((f32[14,64,64]{2,1,0:T(8,128)S(1)}, f32[14,64,64]{2,1,0:T(8,128)S(1)}, u32[]{:S(2)}, u32[]{:S(2)}) %collective-permute-start.18) | collective-permute-done | bytes 229408 | tf_op jit(solution)/shard_map/ppermute | solution.py:16
  201.3 6.9 %collective-permute-done.19 = f32[14,64,64]{2,1,0:T(8,128)S(1)} collective-permute-done((f32[14,64,64]{2,1,0:T(8,128)S(1)}, f32[14,64,64]{2,1,0:T(8,128)S(1)}, u32[]{:S(2)}, u32[]{:S(2)}) %collective-permute-start.19) | collective-permute-done | bytes 229408 | tf_op jit(solution)/shard_map/ppermute | solution.py:16
  212.3 8.4 %copy.89 = f32[16,64,14,64]{1,0,3,2:T(8,128)} copy(f32[16,64,14,64]{1,3,2,0:T(8,128)S(1)} %select_bitcast_fusion) | data formatting | bytes 7340032 | tf_op jit(solution)/shard_map/transpose | solution.py:196
  220.7 7.4 %reshape.575 = f32[1024,896]{0,1:T(8,128)} reshape(f32[16,64,14,64]{1,0,3,2:T(8,128)} %copy.89) | data formatting | bytes 7340032 | tf_op jit(solution)/shard_map/reshape | solution.py:196
  231.9 10.5 %psum.7 = f32[256]{0:T(256)S(1)} all-reduce(f32[256]{0:T(256)S(1)} %get-tuple-element.254), channel_id=1, replica_groups=mesh['seq'=32,'tp'=4] {'tp'}, use_global_device_ids=true, to_apply=%region_6.7 | all-reduce | flops 256 | bytes 2048 | tf_op jit(solution)/shard_map/psum | solution.py:208
  242.6 6.9 %fusion.99 = f32[256,3584]{1,0:T(8,128)} fusion(bf16[256,896]{0,1:T(8,128)(2,1)S(1)} %fusion.41, bf16[896,3584]{1,0:T(8,128)(2,1)} %param.40), kind=kOutput, calls=%fused_computation.324 | convolution fusion | flops 1644167168 | bytes 10551296 | tf_op jit(solution)/shard_map/dot_general | solution.py:215
  251.5 11.2 %collective-permute-done.21 = bf16[2,256,896]{2,1,0:T(8,128)(2,1)} collective-permute-done((bf16[2,256,896]{2,1,0:T(8,128)(2,1)}, bf16[2,256,896]{2,1,0:T(8,128)(2,1)}, u32[]{:S(2)}, u32[]{:S(2)}) %collective-permute-start.21) | collective-permute-done | bytes 917536 | tf_op jit(solution)/shard_map/ppermute | solution.py:16
  264.6 5.9 %collective-permute-start.23 = (bf16[2,256,896]{2,1,0:T(8,128)(2,1)}, bf16[2,256,896]{2,1,0:T(8,128)(2,1)}, u32[]{:S(2)}, u32[]{:S(2)}) collective-permute-start(bf16[2,256,896]{2,1,0:T(8,128)(2,1)} %collective-permute-done.21), channel_id=1, source_target_pairs={{4,0},{8,4},{12,8},{16,12},{20,16},{24,20},{28,24},{32,28},{36,32}... | collective-permute-start | bytes 2752520 | tf_op jit(solution)/shard_map/ppermute | solution.py:16
  274.8 7.0 %collective-permute-done.23 = bf16[2,256,896]{2,1,0:T(8,128)(2,1)} collective-permute-done((bf16[2,256,896]{2,1,0:T(8,128)(2,1)}, bf16[2,256,896]{2,1,0:T(8,128)(2,1)}, u32[]{:S(2)}, u32[]{:S(2)}) %collective-permute-start.23) | collective-permute-done | bytes 917536 | tf_op jit(solution)/shard_map/ppermute | solution.py:16
  281.8 8.1 %collective-permute-done.22 = bf16[4,256,896]{2,1,0:T(8,128)(2,1)} collective-permute-done((bf16[4,256,896]{2,1,0:T(8,128)(2,1)}, bf16[4,256,896]{2,1,0:T(8,128)(2,1)}, u32[]{:S(2)}, u32[]{:S(2)}) %collective-permute-start.22) | collective-permute-done | bytes 1835040 | tf_op jit(solution)/shard_map/ppermute | solution.py:16
  289.9 11.6 %collective-permute-start.24 = (bf16[4,256,896]{2,1,0:T(8,128)(2,1)}, bf16[4,256,896]{2,1,0:T(8,128)(2,1)S(1)}, u32[]{:S(2)}, u32[]{:S(2)}) collective-permute-start(bf16[4,256,896]{2,1,0:T(8,128)(2,1)} %collective-permute-done.22), channel_id=1, source_target_pairs={{0,4},{4,8},{8,12},{12,16},{16,20},{20,24},{24,28},{28,32},{32,36}... | collective-permute-start | bytes 5505032 | tf_op jit(solution)/shard_map/ppermute | solution.py:16
  310.1 5.7 %collective-permute-start.25 = (bf16[2,256,896]{2,1,0:T(8,128)(2,1)}, bf16[2,256,896]{2,1,0:T(8,128)(2,1)S(1)}, u32[]{:S(2)}, u32[]{:S(2)}) collective-permute-start(bf16[2,256,896]{2,1,0:T(8,128)(2,1)} %collective-permute-done.23), channel_id=1, source_target_pairs={{4,0},{8,4},{12,8},{16,12},{20,16},{24,20},{28,24},{32,28},{36,32}... | collective-permute-start | bytes 2752520 | tf_op jit(solution)/shard_map/ppermute | solution.py:16
  337.8 5.8 %collective-permute-start.27 = (bf16[2,256,896]{2,1,0:T(8,128)(2,1)S(1)}, bf16[2,256,896]{2,1,0:T(8,128)(2,1)S(1)}, u32[]{:S(2)}, u32[]{:S(2)}) collective-permute-start(bf16[2,256,896]{2,1,0:T(8,128)(2,1)S(1)} %collective-permute-done.25), channel_id=1, source_target_pairs={{4,0},{8,4},{12,8},{16,12},{20,16},{24,20},{28,24},{32,28},{36,32}... | collective-permute-start | bytes 2752520 | tf_op jit(solution)/shard_map/ppermute | solution.py:16
  383.5 6.2 %all-gather.2.cloned.1.call-done = bf16[256,3584]{1,0:T(8,128)(2,1)} async-done(((bf16[64,3584]{1,0:T(8,128)(2,1)}), bf16[256,3584]{1,0:T(8,128)(2,1)}) %all-gather.2.cloned.1.call-update) | async-done | bytes 1835024 | tf_op jit(solution)/shard_map/all_gather | solution.py:225
  389.7 6.4 %fusion.100 = f32[256,896]{1,0:T(8,128)} fusion(bf16[256,3584]{1,0:T(8,128)(2,1)} %all-gather.2.cloned.1.call-done, bf16[3584,896]{1,0:T(8,128)(2,1)} %param.42), kind=kOutput, calls=%fused_computation.325 | convolution fusion | flops 1644167168 | bytes 9175040 | tf_op jit(solution)/shard_map/dot_general | solution.py:228
  398.7 56.3 %while.2 = (s32[]{:T(128)}, bf16[4,256,224]{1,2,0:T(8,128)(2,1)}, s32[4]{0:T(128)S(1)}, bf16[256,896]{1,0:T(8,128)(2,1)S(1)}, bf16[7424,896]{1,0:T(8,128)(2,1)},...) while((s32[]{:T(128)}, bf16[4,256,224]{1,2,0:T(8,128)(2,1)}, ...), condition=%wide.region_30.31_spmd, body=%wide.region_27.30_spmd.sunk | while | flops 1718148608 | bytes 32561336 | solution.py:281
  400.0 5.3 %fusion.116 = (f32[256]{0:T(256)S(1)}, f32[256,7424]{1,0:T(8,128)S(1)}) fusion(pred[256,7424]{1,0:T(32,128)(4,1)S(1)} %get-tuple-element.368, bf16[7424,896]{1,0:T(8,128)(2,1)} %get-tuple-element.367, s32[]{:T(128)S(6)} %select_n.229, bf16[256,896]{1,0:T(8,128)(2,1)S(1)} %get-tuple-element.366), kind=kOutput, calls=%fused_computation.322.clone.1 | convolution fusion | flops 857145088 | bytes 13436928 | tf_op jit(solution)/shard_map/while/body/eval_jaxpr/dot_general | solution.py:270
  406.5 6.6 %fusion.118 = bf16[4,256,224]{1,2,0:T(8,128)(2,1)} fusion(bf16[4,256,224]{1,2,0:T(8,128)(2,1)} %get-tuple-element.353, s32[]{:T(128)S(6)} %copy.185, bf16[7424,896]{1,0:T(8,128)(2,1)} %get-tuple-element.369, s32[]{:T(128)S(6)} %select_n.229, f32[256,7424]{1,0:T(8,128)S(1)} %get-tuple-element.339, f32[256]{0:T(256)S(1)} %fusion.117, ...), kind=kOutput, calls=%fused_computation.11.clone.1 | convolution fusion | flops 857202688 | bytes 11520008 | tf_op jit(solution)/shard_map/while/body/eval_jaxpr/dot_general | solution.py:279
  420.8 6.6 %fusion.118 = bf16[4,256,224]{1,2,0:T(8,128)(2,1)} fusion(bf16[4,256,224]{1,2,0:T(8,128)(2,1)} %get-tuple-element.353, s32[]{:T(128)S(6)} %copy.185, bf16[7424,896]{1,0:T(8,128)(2,1)} %get-tuple-element.369, s32[]{:T(128)S(6)} %select_n.229, f32[256,7424]{1,0:T(8,128)S(1)} %get-tuple-element.339, f32[256]{0:T(256)S(1)} %fusion.117, ...), kind=kOutput, calls=%fused_computation.11.clone.1 | convolution fusion | flops 857202688 | bytes 11520008 | tf_op jit(solution)/shard_map/while/body/eval_jaxpr/dot_general | solution.py:279
  428.6 5.3 %fusion.116 = (f32[256]{0:T(256)S(1)}, f32[256,7424]{1,0:T(8,128)S(1)}) fusion(pred[256,7424]{1,0:T(32,128)(4,1)S(1)} %get-tuple-element.368, bf16[7424,896]{1,0:T(8,128)(2,1)} %get-tuple-element.367, s32[]{:T(128)S(6)} %select_n.229, bf16[256,896]{1,0:T(8,128)(2,1)S(1)} %get-tuple-element.366), kind=kOutput, calls=%fused_computation.322.clone.1 | convolution fusion | flops 857145088 | bytes 13436928 | tf_op jit(solution)/shard_map/while/body/eval_jaxpr/dot_general | solution.py:270
  435.1 6.6 %fusion.118 = bf16[4,256,224]{1,2,0:T(8,128)(2,1)} fusion(bf16[4,256,224]{1,2,0:T(8,128)(2,1)} %get-tuple-element.353, s32[]{:T(128)S(6)} %copy.185, bf16[7424,896]{1,0:T(8,128)(2,1)} %get-tuple-element.369, s32[]{:T(128)S(6)} %select_n.229, f32[256,7424]{1,0:T(8,128)S(1)} %get-tuple-element.339, f32[256]{0:T(256)S(1)} %fusion.117, ...), kind=kOutput, calls=%fused_computation.11.clone.1 | convolution fusion | flops 857202688 | bytes 11520008 | tf_op jit(solution)/shard_map/while/body/eval_jaxpr/dot_general | solution.py:279
  448.9 6.0 %fusion.118 = bf16[4,256,224]{1,2,0:T(8,128)(2,1)} fusion(bf16[4,256,224]{1,2,0:T(8,128)(2,1)} %get-tuple-element.353, s32[]{:T(128)S(6)} %copy.185, bf16[7424,896]{1,0:T(8,128)(2,1)} %get-tuple-element.369, s32[]{:T(128)S(6)} %select_n.229, f32[256,7424]{1,0:T(8,128)S(1)} %get-tuple-element.339, f32[256]{0:T(256)S(1)} %fusion.117, ...), kind=kOutput, calls=%fused_computation.11.clone.1 | convolution fusion | flops 857202688 | bytes 11520008 | tf_op jit(solution)/shard_map/while/body/eval_jaxpr/dot_general | solution.py:279
  (304 shorter events, 199.8 us)
Async XLA Ops:
  7.2 388.9 %copy-start = (bf16[3584,128]{1,0:T(8,128)(2,1)S(1)}, bf16[3584,128]{1,0:T(8,128)(2,1)}, u32[]{:S(2)}) copy-start(bf16[3584,128]{1,0:T(8,128)(2,1)} %param.43) | copy-start | bytes 2752516
  7.2 350.5 %reduce-scatter.2.cloned.1.call-start = ((), (), s32[]{:S(2)}) async-start(), calls=%async_computation.1 | async-start | bytes 4587520 | tf_op jit(solution)/shard_map/reduce_scatter | solution.py:214
  10.3 40.0 %collective-permute-start = (bf16[4,256,896]{2,1,0:T(8,128)(2,1)}, bf16[4,256,896]{2,1,0:T(8,128)(2,1)}, u32[]{:S(2)}, u32[]{:S(2)}) collective-permute-start(bf16[4,256,896]{2,1,0:T(8,128)(2,1)} %pad_maximum_fusion), channel_id=1, source_target_pairs={{0,4},{4,8},{8,12},{12,16},{16,20},{20,24},{24,28},{28,32},{32,36}... | collective-permute-start | bytes 5505032 | tf_op jit(solution)/shard_map/ppermute | solution.py:16
  14.4 35.8 %collective-permute-start.1 = (bf16[2,256,896]{2,1,0:T(8,128)(2,1)}, bf16[2,256,896]{2,1,0:T(8,128)(2,1)}, u32[]{:S(2)}, u32[]{:S(2)}) collective-permute-start(bf16[2,256,896]{2,1,0:T(8,128)(2,1)} %pad_maximum_fusion.1), channel_id=1, source_target_pairs={{4,0},{8,4},{12,8},{16,12},{20,16},{24,20},{28,24},{32,28},{36,32}... | collective-permute-start | bytes 2752520 | tf_op jit(solution)/shard_map/ppermute | solution.py:16
  20.9 24.7 %collective-permute-start.2 = (bf16[3,896]{1,0:T(4,128)(2,1)S(1)}, bf16[3,896]{1,0:T(4,128)(2,1)}, u32[]{:S(2)}, u32[]{:S(2)}) collective-permute-start(bf16[3,896]{1,0:T(4,128)(2,1)S(1)} %slice.293), channel_id=1, source_target_pairs={{0,4},{4,8},{8,12},{12,16},{16,20},{20,24},{24,28},{28,32},{32,36}... | collective-permute-start | bytes 16136 | tf_op jit(solution)/shard_map/ppermute | solution.py:16
  23.5 20.2 %collective-permute-start.3 = (bf16[3,128]{1,0:T(4,128)(2,1)S(1)}, bf16[3,128]{1,0:T(4,128)(2,1)}, u32[]{:S(2)}, u32[]{:S(2)}) collective-permute-start(bf16[3,128]{1,0:T(4,128)(2,1)S(1)} %slice.304), channel_id=1, source_target_pairs={{0,4},{4,8},{8,12},{12,16},{16,20},{20,24},{24,28},{28,32},{32,36}... | collective-permute-start | bytes 2312 | tf_op jit(solution)/shard_map/ppermute | solution.py:16
  45.7 107.5 %copy-start.29 = (s32[256]{0:T(256)S(1)}, s32[256]{0:T(256)}, u32[]{:S(2)}) copy-start(s32[256]{0:T(256)} %copy-done.28) | copy-start | bytes 3076
  50.3 27.0 %collective-permute-start.4 = (bf16[4,256,896]{2,1,0:T(8,128)(2,1)}, bf16[4,256,896]{2,1,0:T(8,128)(2,1)}, u32[]{:S(2)}, u32[]{:S(2)}) collective-permute-start(bf16[4,256,896]{2,1,0:T(8,128)(2,1)} %collective-permute-done), channel_id=1, source_target_pairs={{0,4},{4,8},{8,12},{12,16},{16,20},{20,24},{24,28},{28,32},{32,36}... | collective-permute-start | bytes 5505032 | tf_op jit(solution)/shard_map/ppermute | solution.py:16
  57.4 16.8 %collective-permute-start.5 = (bf16[2,256,896]{2,1,0:T(8,128)(2,1)}, bf16[2,256,896]{2,1,0:T(8,128)(2,1)}, u32[]{:S(2)}, u32[]{:S(2)}) collective-permute-start(bf16[2,256,896]{2,1,0:T(8,128)(2,1)} %collective-permute-done.1), channel_id=1, source_target_pairs={{4,0},{8,4},{12,8},{16,12},{20,16},{24,20},{28,24},{32,28},{36,32}... | collective-permute-start | bytes 2752520 | tf_op jit(solution)/shard_map/ppermute | solution.py:16
  77.2 32.7 %collective-permute-start.6 = (bf16[4,256,896]{2,1,0:T(8,128)(2,1)}, bf16[4,256,896]{2,1,0:T(8,128)(2,1)}, u32[]{:S(2)}, u32[]{:S(2)}) collective-permute-start(bf16[4,256,896]{2,1,0:T(8,128)(2,1)} %collective-permute-done.4), channel_id=1, source_target_pairs={{0,4},{4,8},{8,12},{12,16},{16,20},{20,24},{24,28},{28,32},{32,36}... | collective-permute-start | bytes 5505032 | tf_op jit(solution)/shard_map/ppermute | solution.py:16
  80.9 29.1 %collective-permute-start.7 = (bf16[2,256,896]{2,1,0:T(8,128)(2,1)}, bf16[2,256,896]{2,1,0:T(8,128)(2,1)}, u32[]{:S(2)}, u32[]{:S(2)}) collective-permute-start(bf16[2,256,896]{2,1,0:T(8,128)(2,1)} %collective-permute-done.5), channel_id=1, source_target_pairs={{4,0},{8,4},{12,8},{16,12},{20,16},{24,20},{28,24},{32,28},{36,32}... | collective-permute-start | bytes 2752520 | tf_op jit(solution)/shard_map/ppermute | solution.py:16
  86.9 22.2 %collective-permute-start.9 = (f32[14,64,64]{2,1,0:T(8,128)S(1)}, f32[14,64,64]{2,1,0:T(8,128)S(1)}, u32[]{:S(2)}, u32[]{:S(2)}) collective-permute-start(f32[14,64,64]{2,1,0:T(8,128)S(1)} %convolution_add_fusion.1), channel_id=1, source_target_pairs={{0,4},{4,8},{8,12},{12,16},{16,20},{20,24},{24,28},{28,32},{32,36}... | collective-permute-start | bytes 688136 | tf_op jit(solution)/shard_map/ppermute | solution.py:16
  88.9 20.2 %collective-permute-start.8 = (f32[14]{0:T(128)S(1)}, f32[14]{0:T(128)S(1)}, u32[]{:S(2)}, u32[]{:S(2)}) collective-permute-start(f32[14]{0:T(128)S(1)} %get-tuple-element.97), channel_id=1, source_target_pairs={{0,4},{4,8},{8,12},{12,16},{16,20},{20,24},{24,28},{28,32},{32,36}... | collective-permute-start | bytes 176 | tf_op jit(solution)/shard_map/ppermute | solution.py:16
  110.0 31.9 %collective-permute-start.10 = (bf16[4,256,896]{2,1,0:T(8,128)(2,1)}, bf16[4,256,896]{2,1,0:T(8,128)(2,1)}, u32[]{:S(2)}, u32[]{:S(2)}) collective-permute-start(bf16[4,256,896]{2,1,0:T(8,128)(2,1)} %collective-permute-done.6), channel_id=1, source_target_pairs={{0,4},{4,8},{8,12},{12,16},{16,20},{20,24},{24,28},{28,32},{32,36}... | collective-permute-start | bytes 5505032 | tf_op jit(solution)/shard_map/ppermute | solution.py:16
  112.5 27.1 %collective-permute-start.11 = (bf16[2,256,896]{2,1,0:T(8,128)(2,1)}, bf16[2,256,896]{2,1,0:T(8,128)(2,1)}, u32[]{:S(2)}, u32[]{:S(2)}) collective-permute-start(bf16[2,256,896]{2,1,0:T(8,128)(2,1)} %collective-permute-done.7), channel_id=1, source_target_pairs={{4,0},{8,4},{12,8},{16,12},{20,16},{24,20},{28,24},{32,28},{36,32}... | collective-permute-start | bytes 2752520 | tf_op jit(solution)/shard_map/ppermute | solution.py:16
  119.8 17.8 %collective-permute-start.13 = (f32[14,64,64]{2,1,0:T(8,128)}, f32[14,64,64]{2,1,0:T(8,128)}, u32[]{:S(2)}, u32[]{:S(2)}) collective-permute-start(f32[14,64,64]{2,1,0:T(8,128)} %multiply_add_fusion.3), channel_id=1, source_target_pairs={{0,8},{4,12},{8,16},{12,20},{16,24},{20,28},{24,32},{28,36},{32,40... | collective-permute-start | bytes 688136 | tf_op jit(solution)/shard_map/ppermute | solution.py:16
  122.6 15.0 %collective-permute-start.12 = (f32[14]{0:T(128)S(1)}, f32[14]{0:T(128)S(1)}, u32[]{:S(2)}, u32[]{:S(2)}) collective-permute-start(f32[14]{0:T(128)S(1)} %mul.384), channel_id=1, source_target_pairs={{0,8},{4,12},{8,16},{12,20},{16,24},{20,28},{24,32},{28,36},{32,40... | collective-permute-start | bytes 176 | tf_op jit(solution)/shard_map/ppermute | solution.py:16
  141.8 39.2 %collective-permute-start.14 = (bf16[4,256,896]{2,1,0:T(8,128)(2,1)}, bf16[4,256,896]{2,1,0:T(8,128)(2,1)}, u32[]{:S(2)}, u32[]{:S(2)}) collective-permute-start(bf16[4,256,896]{2,1,0:T(8,128)(2,1)} %collective-permute-done.10), channel_id=1, source_target_pairs={{0,4},{4,8},{8,12},{12,16},{16,20},{20,24},{24,28},{28,32},{32,36}... | collective-permute-start | bytes 5505032 | tf_op jit(solution)/shard_map/ppermute | solution.py:16
  151.3 29.2 %collective-permute-start.15 = (bf16[2,256,896]{2,1,0:T(8,128)(2,1)}, bf16[2,256,896]{2,1,0:T(8,128)(2,1)}, u32[]{:S(2)}, u32[]{:S(2)}) collective-permute-start(bf16[2,256,896]{2,1,0:T(8,128)(2,1)} %collective-permute-done.11), channel_id=1, source_target_pairs={{4,0},{8,4},{12,8},{16,12},{20,16},{24,20},{28,24},{32,28},{36,32}... | collective-permute-start | bytes 2752520 | tf_op jit(solution)/shard_map/ppermute | solution.py:16
  153.5 25.7 %collective-permute-start.17 = (f32[14,64,64]{2,1,0:T(8,128)}, f32[14,64,64]{2,1,0:T(8,128)}, u32[]{:S(2)}, u32[]{:S(2)}) collective-permute-start(f32[14,64,64]{2,1,0:T(8,128)} %multiply_add_fusion.2), channel_id=1, source_target_pairs={{0,16},{4,20},{8,24},{12,28},{16,32},{20,36},{24,40},{28,44},{32,4... | collective-permute-start | bytes 688136 | tf_op jit(solution)/shard_map/ppermute | solution.py:16
  156.4 22.8 %collective-permute-start.16 = (f32[14]{0:T(128)S(1)}, f32[14]{0:T(128)S(1)}, u32[]{:S(2)}, u32[]{:S(2)}) collective-permute-start(f32[14]{0:T(128)S(1)} %mul.387), channel_id=1, source_target_pairs={{0,16},{4,20},{8,24},{12,28},{16,32},{20,36},{24,40},{28,44},{32,4... | collective-permute-start | bytes 176 | tf_op jit(solution)/shard_map/ppermute | solution.py:16
  181.0 15.1 %collective-permute-start.18 = (f32[14,64,64]{2,1,0:T(8,128)S(1)}, f32[14,64,64]{2,1,0:T(8,128)S(1)}, u32[]{:S(2)}, u32[]{:S(2)}) collective-permute-start(f32[14,64,64]{2,1,0:T(8,128)S(1)} %multiply_add_fusion.1), channel_id=1, source_target_pairs={{0,32},{4,36},{8,40},{12,44},{16,48},{20,52},{24,56},{28,60},{32,6... | collective-permute-start | bytes 688136 | tf_op jit(solution)/shard_map/ppermute | solution.py:16
  196.3 11.9 %collective-permute-start.19 = (f32[14,64,64]{2,1,0:T(8,128)S(1)}, f32[14,64,64]{2,1,0:T(8,128)S(1)}, u32[]{:S(2)}, u32[]{:S(2)}) collective-permute-start(f32[14,64,64]{2,1,0:T(8,128)S(1)} %multiply_add_fusion), channel_id=1, source_target_pairs={{0,4},{4,8},{8,12},{12,16},{16,20},{20,24},{24,28},{28,32},{32,36}... | collective-permute-start | bytes 688136 | tf_op jit(solution)/shard_map/ppermute | solution.py:16
  199.2 63.6 %collective-permute-start.20 = (bf16[4,256,896]{2,1,0:T(8,128)(2,1)}, bf16[4,256,896]{2,1,0:T(8,128)(2,1)}, u32[]{:S(2)}, u32[]{:S(2)}) collective-permute-start(bf16[4,256,896]{2,1,0:T(8,128)(2,1)} %collective-permute-done.14), channel_id=1, source_target_pairs={{0,4},{4,8},{8,12},{12,16},{16,20},{20,24},{24,28},{28,32},{32,36}... | collective-permute-start | bytes 5505032 | tf_op jit(solution)/shard_map/ppermute | solution.py:16
  249.5 140.2 %all-gather.2.cloned.1.call-start = ((), (), s32[]{:S(2)}) async-start(), calls=%async_computation.2 | async-start | bytes 2293760 | tf_op jit(solution)/shard_map/all_gather | solution.py:225
  249.6 13.1 %collective-permute-start.21 = (bf16[2,256,896]{2,1,0:T(8,128)(2,1)}, bf16[2,256,896]{2,1,0:T(8,128)(2,1)}, u32[]{:S(2)}, u32[]{:S(2)}) collective-permute-start(bf16[2,256,896]{2,1,0:T(8,128)(2,1)} %collective-permute-done.15), channel_id=1, source_target_pairs={{4,0},{8,4},{12,8},{16,12},{20,16},{24,20},{28,24},{32,28},{36,32}... | collective-permute-start | bytes 2752520 | tf_op jit(solution)/shard_map/ppermute | solution.py:16
  262.7 27.1 %collective-permute-start.22 = (bf16[4,256,896]{2,1,0:T(8,128)(2,1)}, bf16[4,256,896]{2,1,0:T(8,128)(2,1)}, u32[]{:S(2)}, u32[]{:S(2)}) collective-permute-start(bf16[4,256,896]{2,1,0:T(8,128)(2,1)} %collective-permute-done.20), channel_id=1, source_target_pairs={{0,4},{4,8},{8,12},{12,16},{16,20},{20,24},{24,28},{28,32},{32,36}... | collective-permute-start | bytes 5505032 | tf_op jit(solution)/shard_map/ppermute | solution.py:16
  264.6 17.1 %collective-permute-start.23 = (bf16[2,256,896]{2,1,0:T(8,128)(2,1)}, bf16[2,256,896]{2,1,0:T(8,128)(2,1)}, u32[]{:S(2)}, u32[]{:S(2)}) collective-permute-start(bf16[2,256,896]{2,1,0:T(8,128)(2,1)} %collective-permute-done.21), channel_id=1, source_target_pairs={{4,0},{8,4},{12,8},{16,12},{20,16},{24,20},{28,24},{32,28},{36,32}... | collective-permute-start | bytes 2752520 | tf_op jit(solution)/shard_map/ppermute | solution.py:16
  289.9 37.2 %collective-permute-start.24 = (bf16[4,256,896]{2,1,0:T(8,128)(2,1)}, bf16[4,256,896]{2,1,0:T(8,128)(2,1)S(1)}, u32[]{:S(2)}, u32[]{:S(2)}) collective-permute-start(bf16[4,256,896]{2,1,0:T(8,128)(2,1)} %collective-permute-done.22), channel_id=1, source_target_pairs={{0,4},{4,8},{8,12},{12,16},{16,20},{20,24},{24,28},{28,32},{32,36}... | collective-permute-start | bytes 5505032 | tf_op jit(solution)/shard_map/ppermute | solution.py:16
  310.1 17.0 %collective-permute-start.25 = (bf16[2,256,896]{2,1,0:T(8,128)(2,1)}, bf16[2,256,896]{2,1,0:T(8,128)(2,1)S(1)}, u32[]{:S(2)}, u32[]{:S(2)}) collective-permute-start(bf16[2,256,896]{2,1,0:T(8,128)(2,1)} %collective-permute-done.23), channel_id=1, source_target_pairs={{4,0},{8,4},{12,8},{16,12},{20,16},{24,20},{28,24},{32,28},{36,32}... | collective-permute-start | bytes 2752520 | tf_op jit(solution)/shard_map/ppermute | solution.py:16
  327.1 27.4 %collective-permute-start.26 = (bf16[4,256,896]{2,1,0:T(8,128)(2,1)S(1)}, bf16[4,256,896]{2,1,0:T(8,128)(2,1)S(1)}, u32[]{:S(2)}, u32[]{:S(2)}) collective-permute-start(bf16[4,256,896]{2,1,0:T(8,128)(2,1)S(1)} %collective-permute-done.24), channel_id=1, source_target_pairs={{0,4},{4,8},{8,12},{12,16},{16,20},{20,24},{24,28},{28,32},{32,36}... | collective-permute-start | bytes 5505032 | tf_op jit(solution)/shard_map/ppermute | solution.py:16
  337.8 16.7 %collective-permute-start.27 = (bf16[2,256,896]{2,1,0:T(8,128)(2,1)S(1)}, bf16[2,256,896]{2,1,0:T(8,128)(2,1)S(1)}, u32[]{:S(2)}, u32[]{:S(2)}) collective-permute-start(bf16[2,256,896]{2,1,0:T(8,128)(2,1)S(1)} %collective-permute-done.25), channel_id=1, source_target_pairs={{4,0},{8,4},{12,8},{16,12},{20,16},{24,20},{28,24},{32,28},{36,32}... | collective-permute-start | bytes 2752520 | tf_op jit(solution)/shard_map/ppermute | solution.py:16
  (37 other events, 1206.6 us)
Sparse Core Ops, SparseCore 0:
  249.7 39.0 reduce-scatter.1
  361.1 28.5 all-gather.1
where the time goes:
time: 471 us; the launch traced here: 464 us
  waiting for transfers between devices  113 us (24%)
  starting transfers between devices  103 us (22%)
  local copies, waits for them, and re-layouts  95.2 us (20%)
  matrix products  80.7 us (17%)
  other arithmetic  40 us (8%)
  between operations  18.9 us (4%)
  blocking collectives  10.5 us (2%)
    ppermute x28, waiting for transfers between devices, shifted_2(): lax.ppermute(value, axis, [(source, source + steps) for source in range(i...  107 us
    ppermute x28, starting transfers between devices, shifted_2(): lax.ppermute(value, axis, [(source, source + steps) for source in range(i...  103 us
    unnamed x111, local copies, waits for them, and re-layouts  64.4 us
    dot_general x4, matrix products, attend(): jnp.dot(probs, value_head, preferred_element_type=jnp.float32)  25.8 us
    dot_general x4, matrix products, attend(): lax.dot_general(query_head, key_head, (((1,), (1,)), ((), ())), preferred...  20.6 us
    psum x1, blocking collectives, per_device(): squares = lax.psum(jnp.sum(gated * gated, axis=1), 'tp')  10.5 us
  transfers between devices with their start and end apart: 30, of which 15 were waited for; matrix products, arithmetic and copies ran while one was open for 31% of the time, Pallas kernels for 0%

commit v1 on v0

--- a/solution.py
+++ b/solution.py
@@ -92,18 +92,16 @@
     for distance in range(long_hop, reach + 1):
         relay_steps[distance - long_hop].append((distance, distance - long_hop, long_hop))
 
-    def advance(values, tied=True):
+    def advance(values, tied=True, after=None):
         if not relay_steps or (tied and len(relay_steps) <= reach - tied_steps):
             return values
         moves = relay_steps.pop(0)
         sent = []
         for distance, source, steps in moves:
-            sent.append(
-                (
-                    shifted_2(behind_pieces[source], "seq", steps),
-                    shifted_2(forward_pieces[source], "seq", -steps),
-                )
-            )
+            behind, forward = behind_pieces[source], forward_pieces[source]
+            if after is not None:
+                behind, forward, _ = lax.optimization_barrier((behind, forward, after))
+            sent.append((shifted_2(behind, "seq", steps), shifted_2(forward, "seq", -steps)))
         sent, values = lax.optimization_barrier((sent, values))
         for (distance, _, _), (behind, forward) in zip(moves, sent):
             behind_pieces[distance] = behind
@@ -188,16 +186,19 @@
         distance *= 2
     carried = advance(shifted_2(scan_state, "seq", 1))
     continuing = position[0] > 0
-    replace = (jnp.arange(prompts, dtype=jnp.int32) == segment[0]) & continuing
-    initial = jnp.where(replace[:, None, None, None], carried[None], ssm_cache)
-    selected = (onehot[:, :, None].astype(jnp.bfloat16) * inputs_c[:, None, :]).reshape(
+    first_rows = (segment == segment[0]) & continuing
+    cached_rows = onehot & ~first_rows[:, None]
+    selected = (cached_rows[:, :, None].astype(jnp.bfloat16) * inputs_c[:, None, :]).reshape(
         length, prompts * state_size
     )
-    table = jnp.transpose(initial, (0, 3, 1, 2)).reshape(prompts * state_size, heads * head_size)
+    table = jnp.transpose(ssm_cache, (0, 3, 1, 2)).reshape(prompts * state_size, heads * head_size)
+    carried_table = jnp.transpose(carried, (2, 0, 1)).reshape(state_size, heads * head_size)
+    from_cache = jnp.dot(selected, table, precision=high_precision, preferred_element_type=jnp.float32)
+    from_carried = jnp.dot(
+        inputs_c, carried_table, precision=high_precision, preferred_element_type=jnp.float32
+    )
     init_out = (
-        jnp.dot(
-            selected, table, precision=high_precision, preferred_element_type=jnp.float32
-        ).reshape(length, heads, head_size)
+        jnp.where(first_rows[:, None], from_carried, from_cache).reshape(length, heads, head_size)
         * from_begin[:, :, None]
     )
     mixed = intra_out + init_out + d_skip[None, :, None] * values
@@ -241,7 +242,7 @@
     cache_pieces = [(cache_keys, cache_values, 0)]
     new_pieces = [(new_keys, new_values, 0)]
     while relay_steps:
-        advance((), tied=False)
+        advance((), tied=False, after=attn_in)
     for distance in range(1, reach + 1):
         behind = behind_pieces[distance]
         cache_pieces.append((behind[0], behind[1], -distance))

time: 471 us -> 510 us (1.083)
  the two profiles are of different devices: /device:TPU:16 before, /device:TPU:97 now
where the time goes in v1:
time: 510 us; the launch traced here: 500 us
  waiting for transfers between devices  130 us (25%)
  local copies, waits for them, and re-layouts  99.1 us (19%)
  starting transfers between devices  97.8 us (19%)
  matrix products  81.2 us (16%)
  other arithmetic  61 us (12%)
  between operations  19.3 us (4%)
  blocking collectives  8.69 us (2%)
    ppermute x28, starting transfers between devices, shifted_2(): lax.ppermute(value, axis, [(source, source + steps) for source in range(i...  97.7 us
    ppermute x28, waiting for transfers between devices, shifted_2(): lax.ppermute(value, axis, [(source, source + steps) for source in range(i...  86 us
    unnamed x167, local copies, waits for them, and re-layouts  64 us
    reduce_scatter x1, waiting for transfers between devices, per_device(): lax.psum_scatter(jnp.dot(normed, out_weight, preferred_element_type=jnp.f...  44.4 us
    unnamed x28, other arithmetic  28.8 us
    dot_general x4, matrix products, attend(): jnp.dot(probs, value_head, preferred_element_type=jnp.float32)  25.8 us
    dot_general x4, matrix products, attend(): lax.dot_general(query_head, key_head, (((1,), (1,)), ((), ())), preferred...  20.6 us
    transpose x1, local copies, waits for them, and re-layouts, per_device(): jnp.transpose(ssm_cache, (0, 3, 1, 2))  11.4 us
  transfers between devices with their start and end apart: 30, of which 13 were waited for; matrix products, arithmetic and copies ran while one was open for 29% of the time, Pallas kernels for 0%

profile of v1, /device:TPU:97, one launch (start us, length us, event | category | flops | bytes accessed | tf_op | source)
XLA Modules:
  0.0 500.2 jit_solution(3140267243847008520)
XLA Ops:
  16.5 5.6 %collective-permute-start.2 = (bf16[3,896]{1,0:T(4,128)(2,1)S(1)}, bf16[3,896]{1,0:T(4,128)(2,1)S(1)}, u32[]{:S(2)}, u32[]{:S(2)}) collective-permute-start(bf16[3,896]{1,0:T(4,128)(2,1)S(1)} %slice.293), channel_id=1, source_target_pairs={{0,4},{4,8},{8,12},{12,16},{16,20},{20,24},{24,28},{28,32},{32,36}... | collective-permute-start | bytes 16136 | tf_op jit(solution)/shard_map/ppermute | solution.py:16
  78.1 11.5 %collective-permute-done.5 = bf16[2,256,896]{2,1,0:T(8,128)(2,1)} collective-permute-done((bf16[2,256,896]{2,1,0:T(8,128)(2,1)}, bf16[2,256,896]{2,1,0:T(8,128)(2,1)}, u32[]{:S(2)}, u32[]{:S(2)}) %collective-permute-start.5) | collective-permute-done | bytes 917536 | tf_op jit(solution)/shard_map/ppermute | solution.py:16
  90.5 6.5 %collective-permute-start.6 = (bf16[4,256,896]{2,1,0:T(8,128)(2,1)}, bf16[4,256,896]{2,1,0:T(8,128)(2,1)S(1)}, u32[]{:S(2)}, u32[]{:S(2)}) collective-permute-start(bf16[4,256,896]{2,1,0:T(8,128)(2,1)} %collective-permute-done.4), channel_id=1, source_target_pairs={{0,4},{4,8},{8,12},{12,16},{16,20},{20,24},{24,28},{28,32},{32,36}... | collective-permute-start | bytes 5505032 | tf_op jit(solution)/shard_map/ppermute | solution.py:16
  104.6 5.7 %collective-permute-start.9 = (f32[14,64,64]{2,1,0:T(8,128)S(1)}, f32[14,64,64]{2,1,0:T(8,128)S(1)}, u32[]{:S(2)}, u32[]{:S(2)}) collective-permute-start(f32[14,64,64]{2,1,0:T(8,128)S(1)} %convolution_add_fusion.1), channel_id=1, source_target_pairs={{0,4},{4,8},{8,12},{12,16},{16,20},{20,24},{24,28},{28,32},{32,36}... | collective-permute-start | bytes 688136 | tf_op jit(solution)/shard_map/ppermute | solution.py:16
  113.7 8.7 %collective-permute-done.8 = f32[14]{0:T(128)S(1)} collective-permute-done((f32[14]{0:T(128)S(1)}, f32[14]{0:T(128)S(1)}, u32[]{:S(2)}, u32[]{:S(2)}) %collective-permute-start.8) | collective-permute-done | bytes 88 | tf_op jit(solution)/shard_map/ppermute | solution.py:16
  123.8 6.5 %collective-permute-start.10 = (bf16[4,256,896]{2,1,0:T(8,128)(2,1)S(1)}, bf16[4,256,896]{2,1,0:T(8,128)(2,1)}, u32[]{:S(2)}, u32[]{:S(2)}) collective-permute-start(bf16[4,256,896]{2,1,0:T(8,128)(2,1)S(1)} %collective-permute-done.6), channel_id=1, source_target_pairs={{0,4},{4,8},{8,12},{12,16},{16,20},{20,24},{24,28},{28,32},{32,36}... | collective-permute-start | bytes 5505032 | tf_op jit(solution)/shard_map/ppermute | solution.py:16
  145.7 14.6 %collective-permute-done.12 = f32[14]{0:T(128)S(1)} collective-permute-done((f32[14]{0:T(128)S(1)}, f32[14]{0:T(128)S(1)}, u32[]{:S(2)}, u32[]{:S(2)}) %collective-permute-start.12) | collective-permute-done | bytes 88 | tf_op jit(solution)/shard_map/ppermute | solution.py:16
  172.3 11.4 %copy.92 = f32[16,64,14,64]{1,0,3,2:T(8,128)} copy(f32[16,64,14,64]{1,3,2,0:T(8,128)} %bitcast.204) | data formatting | bytes 7340032 | tf_op jit(solution)/shard_map/transpose | solution.py:194
  183.8 7.3 %reshape.593 = f32[1024,896]{0,1:T(8,128)} reshape(f32[16,64,14,64]{1,0,3,2:T(8,128)} %copy.92) | data formatting | bytes 7340032 | tf_op jit(solution)/shard_map/reshape | solution.py:194
  196.8 6.0 %collective-permute-start.16 = (f32[14]{0:T(128)S(1)}, f32[14]{0:T(128)S(1)}, u32[]{:S(2)}, u32[]{:S(2)}) collective-permute-start(f32[14]{0:T(128)S(1)} %mul.392), channel_id=1, source_target_pairs={{0,16},{4,20},{8,24},{12,28},{16,32},{20,36},{24,40},{28,44},{32,4... | collective-permute-start | bytes 176 | tf_op jit(solution)/shard_map/ppermute | solution.py:16
  203.0 4.3 collective-permute-done.16
  210.7 6.7 %collective-permute-done.18 = f32[14,64,64]{2,1,0:T(8,128)S(1)} collective-permute-done((f32[14,64,64]{2,1,0:T(8,128)S(1)}, f32[14,64,64]{2,1,0:T(8,128)S(1)}, u32[]{:S(2)}, u32[]{:S(2)}) %collective-permute-start.18) | collective-permute-done | bytes 229408 | tf_op jit(solution)/shard_map/ppermute | solution.py:16
  217.6 12.5 %collective-permute-start.19 = (f32[14,64,64]{2,1,0:T(8,128)S(1)}, f32[14,64,64]{2,1,0:T(8,128)S(1)}, u32[]{:S(2)}, u32[]{:S(2)}) collective-permute-start(f32[14,64,64]{2,1,0:T(8,128)S(1)} %multiply_add_fusion), channel_id=1, source_target_pairs={{0,4},{4,8},{8,12},{12,16},{16,20},{20,24},{24,28},{28,32},{32,36}... | collective-permute-start | bytes 688136 | tf_op jit(solution)/shard_map/ppermute | solution.py:16
  237.8 8.7 %psum.7 = f32[256]{0:T(256)S(1)} all-reduce(f32[256]{0:T(256)S(1)} %get-tuple-element.273), channel_id=1, replica_groups=mesh['seq'=32,'tp'=4] {'tp'}, use_global_device_ids=true, to_apply=%region_6.7 | all-reduce | flops 256 | bytes 2048 | tf_op jit(solution)/shard_map/psum | solution.py:209
  246.5 6.8 %fusion.44 = f32[256,3584]{1,0:T(8,128)} fusion(bf16[896,3584]{1,0:T(8,128)(2,1)} %param.40, f32[256,896]{1,0:T(8,128)S(1)} %get-tuple-element.274, f32[896]{0:T(1024)S(1)} %copy-done.13, f32[256]{0:T(256)S(1)} %add_rsqrt_fusion), kind=kOutput, calls=%fused_computation.58 | convolution fusion | flops 1644855296 | bytes 11014656 | tf_op jit(solution)/shard_map/dot_general | solution.py:216
  253.4 44.4 %reduce-scatter.2.cloned.1.call-done = f32[64,3584]{1,0:T(8,128)} async-done(((f32[256,3584]{1,0:T(8,128)}), f32[64,3584]{1,0:T(8,128)}) %reduce-scatter.2.cloned.1.call-update) | async-done | bytes 917520 | tf_op jit(solution)/shard_map/reduce_scatter | solution.py:215
  306.2 15.2 %collective-permute-done.21 = bf16[2,256,896]{2,1,0:T(8,128)(2,1)} collective-permute-done((bf16[2,256,896]{2,1,0:T(8,128)(2,1)}, bf16[2,256,896]{2,1,0:T(8,128)(2,1)}, u32[]{:S(2)}, u32[]{:S(2)}) %collective-permute-start.21) | collective-permute-done | bytes 917536 | tf_op jit(solution)/shard_map/ppermute | solution.py:16
  324.7 6.5 %collective-permute-start.22 = (bf16[4,256,896]{2,1,0:T(8,128)(2,1)}, bf16[4,256,896]{2,1,0:T(8,128)(2,1)}, u32[]{:S(2)}, u32[]{:S(2)}) collective-permute-start(bf16[4,256,896]{2,1,0:T(8,128)(2,1)} %collective-permute-done.20), channel_id=1, source_target_pairs={{0,4},{4,8},{8,12},{12,16},{16,20},{20,24},{24,28},{28,32},{32,36}... | collective-permute-start | bytes 5505032 | tf_op jit(solution)/shard_map/ppermute | solution.py:16
  346.2 6.4 %collective-permute-done.23 = bf16[2,256,896]{2,1,0:T(8,128)(2,1)} collective-permute-done((bf16[2,256,896]{2,1,0:T(8,128)(2,1)}, bf16[2,256,896]{2,1,0:T(8,128)(2,1)}, u32[]{:S(2)}, u32[]{:S(2)}) %collective-permute-start.23) | collective-permute-done | bytes 917536 | tf_op jit(solution)/shard_map/ppermute | solution.py:16
  352.6 5.6 %collective-permute-start.24 = (bf16[4,256,896]{2,1,0:T(8,128)(2,1)}, bf16[4,256,896]{2,1,0:T(8,128)(2,1)}, u32[]{:S(2)}, u32[]{:S(2)}) collective-permute-start(bf16[4,256,896]{2,1,0:T(8,128)(2,1)} %collective-permute-done.22), channel_id=1, source_target_pairs={{0,4},{4,8},{8,12},{12,16},{16,20},{20,24},{24,28},{28,32},{32,36}... | collective-permute-start | bytes 5505032 | tf_op jit(solution)/shard_map/ppermute | solution.py:16
  376.4 6.5 %collective-permute-done.25 = bf16[2,256,896]{2,1,0:T(8,128)(2,1)} collective-permute-done((bf16[2,256,896]{2,1,0:T(8,128)(2,1)}, bf16[2,256,896]{2,1,0:T(8,128)(2,1)}, u32[]{:S(2)}, u32[]{:S(2)}) %collective-permute-start.25) | collective-permute-done | bytes 917536 | tf_op jit(solution)/shard_map/ppermute | solution.py:16
  385.2 6.4 %fusion.106 = f32[256,896]{1,0:T(8,128)} fusion(bf16[256,3584]{1,0:T(8,128)(2,1)} %all-gather.2.cloned.1.call-done, bf16[3584,896]{1,0:T(8,128)(2,1)} %param.42), kind=kOutput, calls=%fused_computation.332 | convolution fusion | flops 1644167168 | bytes 9175040 | tf_op jit(solution)/shard_map/dot_general | solution.py:229
  405.5 5.8 %collective-permute-done.27 = bf16[2,256,896]{2,1,0:T(8,128)(2,1)S(1)} collective-permute-done((bf16[2,256,896]{2,1,0:T(8,128)(2,1)}, bf16[2,256,896]{2,1,0:T(8,128)(2,1)S(1)}, u32[]{:S(2)}, u32[]{:S(2)}) %collective-permute-start.27) | collective-permute-done | bytes 917536 | tf_op jit(solution)/shard_map/ppermute | solution.py:16
  434.7 56.2 %while.2 = (s32[]{:T(128)}, bf16[4,256,224]{1,2,0:T(8,128)(2,1)}, s32[4]{0:T(128)S(1)}, bf16[256,896]{1,0:T(8,128)(2,1)S(1)}, bf16[7424,896]{1,0:T(8,128)(2,1)},...) while((s32[]{:T(128)}, bf16[4,256,224]{1,2,0:T(8,128)(2,1)}, ...), condition=%wide.region_30.31_spmd, body=%wide.region_27.30_spmd.sunk | while | flops 1718148608 | bytes 32561336 | solution.py:282
  435.9 5.3 %fusion.122 = (f32[256]{0:T(256)S(1)}, f32[256,7424]{1,0:T(8,128)S(1)}) fusion(pred[256,7424]{1,0:T(32,128)(4,1)S(1)} %get-tuple-element.387, bf16[7424,896]{1,0:T(8,128)(2,1)} %get-tuple-element.386, s32[]{:T(128)S(6)} %select_n.232, bf16[256,896]{1,0:T(8,128)(2,1)S(1)} %get-tuple-element.385), kind=kOutput, calls=%fused_computation.329.clone.1 | convolution fusion | flops 857145088 | bytes 13436928 | tf_op jit(solution)/shard_map/while/body/eval_jaxpr/dot_general | solution.py:271
  442.4 6.6 %fusion.124 = bf16[4,256,224]{1,2,0:T(8,128)(2,1)} fusion(bf16[4,256,224]{1,2,0:T(8,128)(2,1)} %get-tuple-element.372, s32[]{:T(128)S(6)} %copy.186, bf16[7424,896]{1,0:T(8,128)(2,1)} %get-tuple-element.388, s32[]{:T(128)S(6)} %select_n.232, f32[256,7424]{1,0:T(8,128)S(1)} %get-tuple-element.358, f32[256]{0:T(256)S(1)} %fusion.123, ...), kind=kOutput, calls=%fused_computation.11.clone.1 | convolution fusion | flops 857202688 | bytes 11520008 | tf_op jit(solution)/shard_map/while/body/eval_jaxpr/dot_general | solution.py:280
  450.3 5.3 %fusion.122 = (f32[256]{0:T(256)S(1)}, f32[256,7424]{1,0:T(8,128)S(1)}) fusion(pred[256,7424]{1,0:T(32,128)(4,1)S(1)} %get-tuple-element.387, bf16[7424,896]{1,0:T(8,128)(2,1)} %get-tuple-element.386, s32[]{:T(128)S(6)} %select_n.232, bf16[256,896]{1,0:T(8,128)(2,1)S(1)} %get-tuple-element.385), kind=kOutput, calls=%fused_computation.329.clone.1 | convolution fusion | flops 857145088 | bytes 13436928 | tf_op jit(solution)/shard_map/while/body/eval_jaxpr/dot_general | solution.py:271
  456.8 6.6 %fusion.124 = bf16[4,256,224]{1,2,0:T(8,128)(2,1)} fusion(bf16[4,256,224]{1,2,0:T(8,128)(2,1)} %get-tuple-element.372, s32[]{:T(128)S(6)} %copy.186, bf16[7424,896]{1,0:T(8,128)(2,1)} %get-tuple-element.388, s32[]{:T(128)S(6)} %select_n.232, f32[256,7424]{1,0:T(8,128)S(1)} %get-tuple-element.358, f32[256]{0:T(256)S(1)} %fusion.123, ...), kind=kOutput, calls=%fused_computation.11.clone.1 | convolution fusion | flops 857202688 | bytes 11520008 | tf_op jit(solution)/shard_map/while/body/eval_jaxpr/dot_general | solution.py:280
  464.6 5.3 %fusion.122 = (f32[256]{0:T(256)S(1)}, f32[256,7424]{1,0:T(8,128)S(1)}) fusion(pred[256,7424]{1,0:T(32,128)(4,1)S(1)} %get-tuple-element.387, bf16[7424,896]{1,0:T(8,128)(2,1)} %get-tuple-element.386, s32[]{:T(128)S(6)} %select_n.232, bf16[256,896]{1,0:T(8,128)(2,1)S(1)} %get-tuple-element.385), kind=kOutput, calls=%fused_computation.329.clone.1 | convolution fusion | flops 857145088 | bytes 13436928 | tf_op jit(solution)/shard_map/while/body/eval_jaxpr/dot_general | solution.py:271
  471.1 6.6 %fusion.124 = bf16[4,256,224]{1,2,0:T(8,128)(2,1)} fusion(bf16[4,256,224]{1,2,0:T(8,128)(2,1)} %get-tuple-element.372, s32[]{:T(128)S(6)} %copy.186, bf16[7424,896]{1,0:T(8,128)(2,1)} %get-tuple-element.388, s32[]{:T(128)S(6)} %select_n.232, f32[256,7424]{1,0:T(8,128)S(1)} %get-tuple-element.358, f32[256]{0:T(256)S(1)} %fusion.123, ...), kind=kOutput, calls=%fused_computation.11.clone.1 | convolution fusion | flops 857202688 | bytes 11520008 | tf_op jit(solution)/shard_map/while/body/eval_jaxpr/dot_general | solution.py:280
  478.9 4.7 fusion.122
  484.9 6.0 %fusion.124 = bf16[4,256,224]{1,2,0:T(8,128)(2,1)} fusion(bf16[4,256,224]{1,2,0:T(8,128)(2,1)} %get-tuple-element.372, s32[]{:T(128)S(6)} %copy.186, bf16[7424,896]{1,0:T(8,128)(2,1)} %get-tuple-element.388, s32[]{:T(128)S(6)} %select_n.232, f32[256,7424]{1,0:T(8,128)S(1)} %get-tuple-element.358, f32[256]{0:T(256)S(1)} %fusion.123, ...), kind=kOutput, calls=%fused_computation.11.clone.1 | convolution fusion | flops 857202688 | bytes 11520008 | tf_op jit(solution)/shard_map/while/body/eval_jaxpr/dot_general | solution.py:280
  (363 shorter events, 212.2 us)
Async XLA Ops:
  7.2 384.4 %copy-start = (bf16[3584,128]{1,0:T(8,128)(2,1)S(1)}, bf16[3584,128]{1,0:T(8,128)(2,1)}, u32[]{:S(2)}) copy-start(bf16[3584,128]{1,0:T(8,128)(2,1)} %param.43) | copy-start | bytes 2752516
  7.2 290.6 %reduce-scatter.2.cloned.1.call-start = ((), (), s32[]{:S(2)}) async-start(), calls=%async_computation.1 | async-start | bytes 4587520 | tf_op jit(solution)/shard_map/reduce_scatter | solution.py:215
  9.0 59.1 %collective-permute-start = (bf16[4,256,896]{2,1,0:T(8,128)(2,1)S(1)}, bf16[4,256,896]{2,1,0:T(8,128)(2,1)}, u32[]{:S(2)}, u32[]{:S(2)}) collective-permute-start(bf16[4,256,896]{2,1,0:T(8,128)(2,1)S(1)} %pad_maximum_fusion), channel_id=1, source_target_pairs={{0,4},{4,8},{8,12},{12,16},{16,20},{20,24},{24,28},{28,32},{32,36}... | collective-permute-start | bytes 5505032 | tf_op jit(solution)/shard_map/ppermute | solution.py:16
  13.7 54.5 %collective-permute-start.1 = (bf16[2,256,896]{2,1,0:T(8,128)(2,1)}, bf16[2,256,896]{2,1,0:T(8,128)(2,1)}, u32[]{:S(2)}, u32[]{:S(2)}) collective-permute-start(bf16[2,256,896]{2,1,0:T(8,128)(2,1)} %pad_maximum_fusion.1), channel_id=1, source_target_pairs={{4,0},{8,4},{12,8},{16,12},{20,16},{24,20},{28,24},{32,28},{36,32}... | collective-permute-start | bytes 2752520 | tf_op jit(solution)/shard_map/ppermute | solution.py:16
  16.5 46.9 %collective-permute-start.2 = (bf16[3,896]{1,0:T(4,128)(2,1)S(1)}, bf16[3,896]{1,0:T(4,128)(2,1)S(1)}, u32[]{:S(2)}, u32[]{:S(2)}) collective-permute-start(bf16[3,896]{1,0:T(4,128)(2,1)S(1)} %slice.293), channel_id=1, source_target_pairs={{0,4},{4,8},{8,12},{12,16},{16,20},{20,24},{24,28},{28,32},{32,36}... | collective-permute-start | bytes 16136 | tf_op jit(solution)/shard_map/ppermute | solution.py:16
  22.7 38.6 %collective-permute-start.3 = (bf16[3,128]{1,0:T(4,128)(2,1)S(1)}, bf16[3,128]{1,0:T(4,128)(2,1)}, u32[]{:S(2)}, u32[]{:S(2)}) collective-permute-start(bf16[3,128]{1,0:T(4,128)(2,1)S(1)} %slice.304), channel_id=1, source_target_pairs={{0,4},{4,8},{8,12},{12,16},{16,20},{20,24},{24,28},{28,32},{32,36}... | collective-permute-start | bytes 2312 | tf_op jit(solution)/shard_map/ppermute | solution.py:16
  68.1 102.8 %copy-start.52 = (f32[14]{0:T(128)S(1)}, f32[14]{0:T(128)}, u32[]{:S(2)}) copy-start(f32[14]{0:T(128)} %param.38) | copy-start | bytes 172
  68.1 22.4 %collective-permute-start.4 = (bf16[4,256,896]{2,1,0:T(8,128)(2,1)}, bf16[4,256,896]{2,1,0:T(8,128)(2,1)}, u32[]{:S(2)}, u32[]{:S(2)}) collective-permute-start(bf16[4,256,896]{2,1,0:T(8,128)(2,1)} %collective-permute-done), channel_id=1, source_target_pairs={{0,4},{4,8},{8,12},{12,16},{16,20},{20,24},{24,28},{28,32},{32,36}... | collective-permute-start | bytes 5505032 | tf_op jit(solution)/shard_map/ppermute | solution.py:16
  72.4 17.1 %collective-permute-start.5 = (bf16[2,256,896]{2,1,0:T(8,128)(2,1)}, bf16[2,256,896]{2,1,0:T(8,128)(2,1)}, u32[]{:S(2)}, u32[]{:S(2)}) collective-permute-start(bf16[2,256,896]{2,1,0:T(8,128)(2,1)} %collective-permute-done.1), channel_id=1, source_target_pairs={{4,0},{8,4},{12,8},{16,12},{20,16},{24,20},{28,24},{32,28},{36,32}... | collective-permute-start | bytes 2752520 | tf_op jit(solution)/shard_map/ppermute | solution.py:16
  90.5 32.0 %collective-permute-start.6 = (bf16[4,256,896]{2,1,0:T(8,128)(2,1)}, bf16[4,256,896]{2,1,0:T(8,128)(2,1)S(1)}, u32[]{:S(2)}, u32[]{:S(2)}) collective-permute-start(bf16[4,256,896]{2,1,0:T(8,128)(2,1)} %collective-permute-done.4), channel_id=1, source_target_pairs={{0,4},{4,8},{8,12},{12,16},{16,20},{20,24},{24,28},{28,32},{32,36}... | collective-permute-start | bytes 5505032 | tf_op jit(solution)/shard_map/ppermute | solution.py:16
  101.3 21.2 %collective-permute-start.7 = (bf16[2,256,896]{2,1,0:T(8,128)(2,1)}, bf16[2,256,896]{2,1,0:T(8,128)(2,1)S(1)}, u32[]{:S(2)}, u32[]{:S(2)}) collective-permute-start(bf16[2,256,896]{2,1,0:T(8,128)(2,1)} %collective-permute-done.5), channel_id=1, source_target_pairs={{4,0},{8,4},{12,8},{16,12},{20,16},{24,20},{28,24},{32,28},{36,32}... | collective-permute-start | bytes 2752520 | tf_op jit(solution)/shard_map/ppermute | solution.py:16
  104.6 17.8 %collective-permute-start.9 = (f32[14,64,64]{2,1,0:T(8,128)S(1)}, f32[14,64,64]{2,1,0:T(8,128)S(1)}, u32[]{:S(2)}, u32[]{:S(2)}) collective-permute-start(f32[14,64,64]{2,1,0:T(8,128)S(1)} %convolution_add_fusion.1), channel_id=1, source_target_pairs={{0,4},{4,8},{8,12},{12,16},{16,20},{20,24},{24,28},{28,32},{32,36}... | collective-permute-start | bytes 688136 | tf_op jit(solution)/shard_map/ppermute | solution.py:16
  111.0 11.4 %collective-permute-start.8 = (f32[14]{0:T(128)S(1)}, f32[14]{0:T(128)S(1)}, u32[]{:S(2)}, u32[]{:S(2)}) collective-permute-start(f32[14]{0:T(128)S(1)} %get-tuple-element.105), channel_id=1, source_target_pairs={{0,4},{4,8},{8,12},{12,16},{16,20},{20,24},{24,28},{28,32},{32,36}... | collective-permute-start | bytes 176 | tf_op jit(solution)/shard_map/ppermute | solution.py:16
  123.8 36.7 %collective-permute-start.10 = (bf16[4,256,896]{2,1,0:T(8,128)(2,1)S(1)}, bf16[4,256,896]{2,1,0:T(8,128)(2,1)}, u32[]{:S(2)}, u32[]{:S(2)}) collective-permute-start(bf16[4,256,896]{2,1,0:T(8,128)(2,1)S(1)} %collective-permute-done.6), channel_id=1, source_target_pairs={{0,4},{4,8},{8,12},{12,16},{16,20},{20,24},{24,28},{28,32},{32,36}... | collective-permute-start | bytes 5505032 | tf_op jit(solution)/shard_map/ppermute | solution.py:16
  135.4 25.0 %collective-permute-start.11 = (bf16[2,256,896]{2,1,0:T(8,128)(2,1)S(1)}, bf16[2,256,896]{2,1,0:T(8,128)(2,1)}, u32[]{:S(2)}, u32[]{:S(2)}) collective-permute-start(bf16[2,256,896]{2,1,0:T(8,128)(2,1)S(1)} %collective-permute-done.7), channel_id=1, source_target_pairs={{4,0},{8,4},{12,8},{16,12},{20,16},{24,20},{28,24},{32,28},{36,32}... | collective-permute-start | bytes 2752520 | tf_op jit(solution)/shard_map/ppermute | solution.py:16
  138.8 21.5 %collective-permute-start.13 = (f32[14,64,64]{2,1,0:T(8,128)S(1)}, f32[14,64,64]{2,1,0:T(8,128)S(1)}, u32[]{:S(2)}, u32[]{:S(2)}) collective-permute-start(f32[14,64,64]{2,1,0:T(8,128)S(1)} %multiply_add_fusion.3), channel_id=1, source_target_pairs={{0,8},{4,12},{8,16},{12,20},{16,24},{20,28},{24,32},{28,36},{32,40... | collective-permute-start | bytes 688136 | tf_op jit(solution)/shard_map/ppermute | solution.py:16
  142.3 18.0 %collective-permute-start.12 = (f32[14]{0:T(128)S(1)}, f32[14]{0:T(128)S(1)}, u32[]{:S(2)}, u32[]{:S(2)}) collective-permute-start(f32[14]{0:T(128)S(1)} %mul.389), channel_id=1, source_target_pairs={{0,8},{4,12},{8,16},{12,20},{16,24},{20,28},{24,32},{28,36},{32,40... | collective-permute-start | bytes 176 | tf_op jit(solution)/shard_map/ppermute | solution.py:16
  160.4 48.0 %collective-permute-start.14 = (bf16[4,256,896]{2,1,0:T(8,128)(2,1)}, bf16[4,256,896]{2,1,0:T(8,128)(2,1)}, u32[]{:S(2)}, u32[]{:S(2)}) collective-permute-start(bf16[4,256,896]{2,1,0:T(8,128)(2,1)} %collective-permute-done.10), channel_id=1, source_target_pairs={{0,4},{4,8},{8,12},{12,16},{16,20},{20,24},{24,28},{28,32},{32,36}... | collective-permute-start | bytes 5505032 | tf_op jit(solution)/shard_map/ppermute | solution.py:16
  168.3 40.1 %collective-permute-start.15 = (bf16[2,256,896]{2,1,0:T(8,128)(2,1)}, bf16[2,256,896]{2,1,0:T(8,128)(2,1)}, u32[]{:S(2)}, u32[]{:S(2)}) collective-permute-start(bf16[2,256,896]{2,1,0:T(8,128)(2,1)} %collective-permute-done.11), channel_id=1, source_target_pairs={{4,0},{8,4},{12,8},{16,12},{20,16},{24,20},{28,24},{32,28},{36,32}... | collective-permute-start | bytes 2752520 | tf_op jit(solution)/shard_map/ppermute | solution.py:16
  191.6 15.7 %collective-permute-start.17 = (f32[14,64,64]{2,1,0:T(8,128)S(1)}, f32[14,64,64]{2,1,0:T(8,128)}, u32[]{:S(2)}, u32[]{:S(2)}) collective-permute-start(f32[14,64,64]{2,1,0:T(8,128)S(1)} %multiply_add_fusion.2), channel_id=1, source_target_pairs={{0,16},{4,20},{8,24},{12,28},{16,32},{20,36},{24,40},{28,44},{32,4... | collective-permute-start | bytes 688136 | tf_op jit(solution)/shard_map/ppermute | solution.py:16
  196.8 10.4 %collective-permute-start.16 = (f32[14]{0:T(128)S(1)}, f32[14]{0:T(128)S(1)}, u32[]{:S(2)}, u32[]{:S(2)}) collective-permute-start(f32[14]{0:T(128)S(1)} %mul.392), channel_id=1, source_target_pairs={{0,16},{4,20},{8,24},{12,28},{16,32},{20,36},{24,40},{28,44},{32,4... | collective-permute-start | bytes 176 | tf_op jit(solution)/shard_map/ppermute | solution.py:16
  208.4 9.0 %collective-permute-start.18 = (f32[14,64,64]{2,1,0:T(8,128)S(1)}, f32[14,64,64]{2,1,0:T(8,128)S(1)}, u32[]{:S(2)}, u32[]{:S(2)}) collective-permute-start(f32[14,64,64]{2,1,0:T(8,128)S(1)} %multiply_add_fusion.1), channel_id=1, source_target_pairs={{0,32},{4,36},{8,40},{12,44},{16,48},{20,52},{24,56},{28,60},{32,6... | collective-permute-start | bytes 688136 | tf_op jit(solution)/shard_map/ppermute | solution.py:16
  217.6 17.9 %collective-permute-start.19 = (f32[14,64,64]{2,1,0:T(8,128)S(1)}, f32[14,64,64]{2,1,0:T(8,128)S(1)}, u32[]{:S(2)}, u32[]{:S(2)}) collective-permute-start(f32[14,64,64]{2,1,0:T(8,128)S(1)} %multiply_add_fusion), channel_id=1, source_target_pairs={{0,4},{4,8},{8,12},{12,16},{16,20},{20,24},{24,28},{28,32},{32,36}... | collective-permute-start | bytes 688136 | tf_op jit(solution)/shard_map/ppermute | solution.py:16
  253.3 131.8 %all-gather.2.cloned.1.call-start = ((), (), s32[]{:S(2)}) async-start(), calls=%async_computation.2 | async-start | bytes 2293760 | tf_op jit(solution)/shard_map/all_gather | solution.py:226
  300.9 23.8 %collective-permute-start.20 = (bf16[4,256,896]{2,1,0:T(8,128)(2,1)}, bf16[4,256,896]{2,1,0:T(8,128)(2,1)}, u32[]{:S(2)}, u32[]{:S(2)}) collective-permute-start(bf16[4,256,896]{2,1,0:T(8,128)(2,1)} %collective-permute-done.14), channel_id=1, source_target_pairs={{0,4},{4,8},{8,12},{12,16},{16,20},{20,24},{24,28},{28,32},{32,36}... | collective-permute-start | bytes 5505032 | tf_op jit(solution)/shard_map/ppermute | solution.py:16
  304.3 17.1 %collective-permute-start.21 = (bf16[2,256,896]{2,1,0:T(8,128)(2,1)}, bf16[2,256,896]{2,1,0:T(8,128)(2,1)}, u32[]{:S(2)}, u32[]{:S(2)}) collective-permute-start(bf16[2,256,896]{2,1,0:T(8,128)(2,1)} %collective-permute-done.15), channel_id=1, source_target_pairs={{4,0},{8,4},{12,8},{16,12},{20,16},{24,20},{28,24},{32,28},{36,32}... | collective-permute-start | bytes 2752520 | tf_op jit(solution)/shard_map/ppermute | solution.py:16
  324.7 27.8 %collective-permute-start.22 = (bf16[4,256,896]{2,1,0:T(8,128)(2,1)}, bf16[4,256,896]{2,1,0:T(8,128)(2,1)}, u32[]{:S(2)}, u32[]{:S(2)}) collective-permute-start(bf16[4,256,896]{2,1,0:T(8,128)(2,1)} %collective-permute-done.20), channel_id=1, source_target_pairs={{0,4},{4,8},{8,12},{12,16},{16,20},{20,24},{24,28},{28,32},{32,36}... | collective-permute-start | bytes 5505032 | tf_op jit(solution)/shard_map/ppermute | solution.py:16
  335.4 17.1 %collective-permute-start.23 = (bf16[2,256,896]{2,1,0:T(8,128)(2,1)}, bf16[2,256,896]{2,1,0:T(8,128)(2,1)}, u32[]{:S(2)}, u32[]{:S(2)}) collective-permute-start(bf16[2,256,896]{2,1,0:T(8,128)(2,1)} %collective-permute-done.21), channel_id=1, source_target_pairs={{4,0},{8,4},{12,8},{16,12},{20,16},{24,20},{28,24},{32,28},{36,32}... | collective-permute-start | bytes 2752520 | tf_op jit(solution)/shard_map/ppermute | solution.py:16
  352.6 30.3 %collective-permute-start.24 = (bf16[4,256,896]{2,1,0:T(8,128)(2,1)}, bf16[4,256,896]{2,1,0:T(8,128)(2,1)}, u32[]{:S(2)}, u32[]{:S(2)}) collective-permute-start(bf16[4,256,896]{2,1,0:T(8,128)(2,1)} %collective-permute-done.22), channel_id=1, source_target_pairs={{0,4},{4,8},{8,12},{12,16},{16,20},{20,24},{24,28},{28,32},{32,36}... | collective-permute-start | bytes 5505032 | tf_op jit(solution)/shard_map/ppermute | solution.py:16
  365.7 17.1 %collective-permute-start.25 = (bf16[2,256,896]{2,1,0:T(8,128)(2,1)}, bf16[2,256,896]{2,1,0:T(8,128)(2,1)}, u32[]{:S(2)}, u32[]{:S(2)}) collective-permute-start(bf16[2,256,896]{2,1,0:T(8,128)(2,1)} %collective-permute-done.23), channel_id=1, source_target_pairs={{4,0},{8,4},{12,8},{16,12},{20,16},{24,20},{28,24},{32,28},{36,32}... | collective-permute-start | bytes 2752520 | tf_op jit(solution)/shard_map/ppermute | solution.py:16
  382.9 28.5 %collective-permute-start.26 = (bf16[4,256,896]{2,1,0:T(8,128)(2,1)}, bf16[4,256,896]{2,1,0:T(8,128)(2,1)}, u32[]{:S(2)}, u32[]{:S(2)}) collective-permute-start(bf16[4,256,896]{2,1,0:T(8,128)(2,1)} %collective-permute-done.24), channel_id=1, source_target_pairs={{0,4},{4,8},{8,12},{12,16},{16,20},{20,24},{24,28},{28,32},{32,36}... | collective-permute-start | bytes 5505032 | tf_op jit(solution)/shard_map/ppermute | solution.py:16
  394.2 17.2 %collective-permute-start.27 = (bf16[2,256,896]{2,1,0:T(8,128)(2,1)}, bf16[2,256,896]{2,1,0:T(8,128)(2,1)S(1)}, u32[]{:S(2)}, u32[]{:S(2)}) collective-permute-start(bf16[2,256,896]{2,1,0:T(8,128)(2,1)} %collective-permute-done.25), channel_id=1, source_target_pairs={{4,0},{8,4},{12,8},{16,12},{20,16},{24,20},{28,24},{32,28},{36,32}... | collective-permute-start | bytes 2752520 | tf_op jit(solution)/shard_map/ppermute | solution.py:16
  (65 other events, 1768.0 us)
Sparse Core Ops, SparseCore 0:
  253.4 44.3 reduce-scatter.1
  339.7 28.1 all-gather.1

commit v2 on v0

--- a/solution.py
+++ b/solution.py
@@ -83,7 +83,7 @@
     reach = seq_count // 4 + 1
     first = seq_index * length
     long_hop = reach + 1
-    tied_steps = 5
+    tied_steps = 9
     behind_pieces = [jnp.stack([cache_keys, cache_values, new_keys, new_values])] * (reach + 1)
     forward_pieces = [jnp.stack([cache_keys, cache_values])] * (reach + 1)
     relay_steps = []
@@ -104,7 +104,7 @@
                     shifted_2(forward_pieces[source], "seq", -steps),
                 )
             )
-        sent, values = lax.optimization_barrier((sent, values))
+        _, values = lax.optimization_barrier((sent, values))
         for (distance, _, _), (behind, forward) in zip(moves, sent):
             behind_pieces[distance] = behind
             forward_pieces[distance] = forward

time: 471 us -> 486 us (1.032)
  waiting for transfers between devices: 113 us -> 131 us
  starting transfers between devices: 103 us -> 110 us
  other arithmetic: 40 us -> 35.1 us
    ppermute x28, waiting for transfers between devices: 107 us -> 128 us  [shifted_2(): lax.ppermute(value, axis, [(source, source + steps) for source in range(i...]
    ppermute x28, starting transfers between devices: 103 us -> 109 us  [shifted_2(): lax.ppermute(value, axis, [(source, source + steps) for source in range(i...]
    unnamed x111 -> x67, local copies, waits for them, and re-layouts: 64.4 us -> 66 us
  transfers between devices with their start and end apart: 30 -> 30, of which waited for: 15 -> 12; matrix products, arithmetic and copies ran while one was open for 31% -> 28% of each run, Pallas kernels for 0% -> 0%
where the time goes in v2:
time: 486 us; the launch traced here: 482 us
  waiting for transfers between devices  131 us (27%)
  starting transfers between devices  110 us (23%)
  local copies, waits for them, and re-layouts  95.4 us (20%)
  matrix products  79.5 us (16%)
  other arithmetic  35.1 us (7%)
  between operations  18.5 us (4%)
  blocking collectives  10.5 us (2%)
    ppermute x28, waiting for transfers between devices, shifted_2(): lax.ppermute(value, axis, [(source, source + steps) for source in range(i...  128 us
    ppermute x28, starting transfers between devices, shifted_2(): lax.ppermute(value, axis, [(source, source + steps) for source in range(i...  109 us
    unnamed x67, local copies, waits for them, and re-layouts  66 us
    dot_general x4, matrix products, attend(): jnp.dot(probs, value_head, preferred_element_type=jnp.float32)  25.8 us
    dot_general x4, matrix products, attend(): lax.dot_general(query_head, key_head, (((1,), (1,)), ((), ())), preferred...  20.8 us
    psum x1, blocking collectives, per_device(): squares = lax.psum(jnp.sum(gated * gated, axis=1), 'tp')  10.5 us
  transfers between devices with their start and end apart: 30, of which 12 were waited for; matrix products, arithmetic and copies ran while one was open for 28% of the time, Pallas kernels for 0%

profile of v2, /device:TPU:16, one launch (start us, length us, event | category | flops | bytes accessed | tf_op | source)
XLA Modules:
  0.0 482.1 jit_solution(12982480033212972941)
XLA Ops:
  13.2 5.7 %collective-permute-start.9 = (bf16[2,256,896]{2,1,0:T(8,128)(2,1)}, bf16[2,256,896]{2,1,0:T(8,128)(2,1)}, u32[]{:S(2)}, u32[]{:S(2)}) collective-permute-start(bf16[2,256,896]{2,1,0:T(8,128)(2,1)} %pad_maximum_fusion.1), channel_id=1, source_target_pairs={{4,0},{8,4},{12,8},{16,12},{20,16},{24,20},{28,24},{32,28},{36,32}... | collective-permute-start | bytes 2752520 | tf_op jit(solution)/shard_map/ppermute | solution.py:16
  39.2 23.6 %collective-permute-done.1 = bf16[4,256,896]{2,1,0:T(8,128)(2,1)} collective-permute-done((bf16[4,256,896]{2,1,0:T(8,128)(2,1)}, bf16[4,256,896]{2,1,0:T(8,128)(2,1)}, u32[]{:S(2)}, u32[]{:S(2)}) %collective-permute-start.1) | collective-permute-done | bytes 1835040 | tf_op jit(solution)/shard_map/ppermute | solution.py:16
  66.5 23.2 %collective-permute-done.2 = bf16[4,256,896]{2,1,0:T(8,128)(2,1)S(1)} collective-permute-done((bf16[4,256,896]{2,1,0:T(8,128)(2,1)}, bf16[4,256,896]{2,1,0:T(8,128)(2,1)S(1)}, u32[]{:S(2)}, u32[]{:S(2)}) %collective-permute-start.2) | collective-permute-done | bytes 1835040 | tf_op jit(solution)/shard_map/ppermute | solution.py:16
  94.4 22.0 %collective-permute-done.3 = bf16[4,256,896]{2,1,0:T(8,128)(2,1)} collective-permute-done((bf16[4,256,896]{2,1,0:T(8,128)(2,1)S(1)}, bf16[4,256,896]{2,1,0:T(8,128)(2,1)}, u32[]{:S(2)}, u32[]{:S(2)}) %collective-permute-start.3) | collective-permute-done | bytes 1835040 | tf_op jit(solution)/shard_map/ppermute | solution.py:16
  120.2 5.8 %collective-permute-start.10 = (bf16[2,256,896]{2,1,0:T(8,128)(2,1)}, bf16[2,256,896]{2,1,0:T(8,128)(2,1)}, u32[]{:S(2)}, u32[]{:S(2)}) collective-permute-start(bf16[2,256,896]{2,1,0:T(8,128)(2,1)} %collective-permute-done.9), channel_id=1, source_target_pairs={{4,0},{8,4},{12,8},{16,12},{20,16},{24,20},{28,24},{32,28},{36,32}... | collective-permute-start | bytes 2752520 | tf_op jit(solution)/shard_map/ppermute | solution.py:16
  127.6 9.6 %collective-permute-done.10 = bf16[2,256,896]{2,1,0:T(8,128)(2,1)} collective-permute-done((bf16[2,256,896]{2,1,0:T(8,128)(2,1)}, bf16[2,256,896]{2,1,0:T(8,128)(2,1)}, u32[]{:S(2)}, u32[]{:S(2)}) %collective-permute-start.10) | collective-permute-done | bytes 917536 | tf_op jit(solution)/shard_map/ppermute | solution.py:16
  137.2 5.9 %collective-permute-start.11 = (bf16[2,256,896]{2,1,0:T(8,128)(2,1)}, bf16[2,256,896]{2,1,0:T(8,128)(2,1)}, u32[]{:S(2)}, u32[]{:S(2)}) collective-permute-start(bf16[2,256,896]{2,1,0:T(8,128)(2,1)} %collective-permute-done.10), channel_id=1, source_target_pairs={{4,0},{8,4},{12,8},{16,12},{20,16},{24,20},{28,24},{32,28},{36,32}... | collective-permute-start | bytes 2752520 | tf_op jit(solution)/shard_map/ppermute | solution.py:16
  146.8 7.5 %collective-permute-done.11 = bf16[2,256,896]{2,1,0:T(8,128)(2,1)} collective-permute-done((bf16[2,256,896]{2,1,0:T(8,128)(2,1)}, bf16[2,256,896]{2,1,0:T(8,128)(2,1)}, u32[]{:S(2)}, u32[]{:S(2)}) %collective-permute-start.11) | collective-permute-done | bytes 917536 | tf_op jit(solution)/shard_map/ppermute | solution.py:16
  154.3 5.9 %collective-permute-start.12 = (bf16[2,256,896]{2,1,0:T(8,128)(2,1)}, bf16[2,256,896]{2,1,0:T(8,128)(2,1)}, u32[]{:S(2)}, u32[]{:S(2)}) collective-permute-start(bf16[2,256,896]{2,1,0:T(8,128)(2,1)} %collective-permute-done.11), channel_id=1, source_target_pairs={{4,0},{8,4},{12,8},{16,12},{20,16},{24,20},{28,24},{32,28},{36,32}... | collective-permute-start | bytes 2752520 | tf_op jit(solution)/shard_map/ppermute | solution.py:16
  162.0 9.5 %collective-permute-done.12 = bf16[2,256,896]{2,1,0:T(8,128)(2,1)} collective-permute-done((bf16[2,256,896]{2,1,0:T(8,128)(2,1)}, bf16[2,256,896]{2,1,0:T(8,128)(2,1)}, u32[]{:S(2)}, u32[]{:S(2)}) %collective-permute-start.12) | collective-permute-done | bytes 917536 | tf_op jit(solution)/shard_map/ppermute | solution.py:16
  171.4 5.9 %collective-permute-start.13 = (bf16[2,256,896]{2,1,0:T(8,128)(2,1)}, bf16[2,256,896]{2,1,0:T(8,128)(2,1)}, u32[]{:S(2)}, u32[]{:S(2)}) collective-permute-start(bf16[2,256,896]{2,1,0:T(8,128)(2,1)} %collective-permute-done.12), channel_id=1, source_target_pairs={{4,0},{8,4},{12,8},{16,12},{20,16},{24,20},{28,24},{32,28},{36,32}... | collective-permute-start | bytes 2752520 | tf_op jit(solution)/shard_map/ppermute | solution.py:16
  183.6 5.0 %collective-permute-done.13 = bf16[2,256,896]{2,1,0:T(8,128)(2,1)} collective-permute-done((bf16[2,256,896]{2,1,0:T(8,128)(2,1)}, bf16[2,256,896]{2,1,0:T(8,128)(2,1)}, u32[]{:S(2)}, u32[]{:S(2)}) %collective-permute-start.13) | collective-permute-done | bytes 917536 | tf_op jit(solution)/shard_map/ppermute | solution.py:16
  188.6 5.9 %collective-permute-start.14 = (bf16[2,256,896]{2,1,0:T(8,128)(2,1)}, bf16[2,256,896]{2,1,0:T(8,128)(2,1)}, u32[]{:S(2)}, u32[]{:S(2)}) collective-permute-start(bf16[2,256,896]{2,1,0:T(8,128)(2,1)} %collective-permute-done.13), channel_id=1, source_target_pairs={{4,0},{8,4},{12,8},{16,12},{20,16},{24,20},{28,24},{32,28},{36,32}... | collective-permute-start | bytes 2752520 | tf_op jit(solution)/shard_map/ppermute | solution.py:16
  207.8 6.1 %collective-permute-done.20 = f32[14]{0:T(128)S(1)} collective-permute-done((f32[14]{0:T(128)S(1)}, f32[14]{0:T(128)S(1)}, u32[]{:S(2)}, u32[]{:S(2)}) %collective-permute-start.20) | collective-permute-done | bytes 88 | tf_op jit(solution)/shard_map/ppermute | solution.py:16
  225.2 10.8 %collective-permute-done.22 = f32[14]{0:T(128)S(1)} collective-permute-done((f32[14]{0:T(128)S(1)}, f32[14]{0:T(128)S(1)}, u32[]{:S(2)}, u32[]{:S(2)}) %collective-permute-start.22) | collective-permute-done | bytes 88 | tf_op jit(solution)/shard_map/ppermute | solution.py:16
  239.3 6.1 %collective-permute-start.24 = (f32[14]{0:T(128)S(1)}, f32[14]{0:T(128)S(1)}, u32[]{:S(2)}, u32[]{:S(2)}) collective-permute-start(f32[14]{0:T(128)S(1)} %mul.387), channel_id=1, source_target_pairs={{0,16},{4,20},{8,24},{12,28},{16,32},{20,36},{24,40},{28,44},{32,4... | collective-permute-start | bytes 176 | tf_op jit(solution)/shard_map/ppermute | solution.py:16
  245.5 23.5 %collective-permute-start.16 = (bf16[2,256,896]{2,1,0:T(8,128)(2,1)}, bf16[2,256,896]{2,1,0:T(8,128)(2,1)}, u32[]{:S(2)}, u32[]{:S(2)}) collective-permute-start(bf16[2,256,896]{2,1,0:T(8,128)(2,1)} %collective-permute-done.15), channel_id=1, source_target_pairs={{4,0},{8,4},{12,8},{16,12},{20,16},{24,20},{28,24},{32,28},{36,32}... | collective-permute-start | bytes 2752520 | tf_op jit(solution)/shard_map/ppermute | solution.py:16
  274.2 8.5 %collective-permute-done.26 = f32[14,64,64]{2,1,0:T(8,128)S(1)} collective-permute-done((f32[14,64,64]{2,1,0:T(8,128)S(1)}, f32[14,64,64]{2,1,0:T(8,128)S(1)}, u32[]{:S(2)}, u32[]{:S(2)}) %collective-permute-start.26) | collective-permute-done | bytes 229408 | tf_op jit(solution)/shard_map/ppermute | solution.py:16
  289.2 5.9 %collective-permute-start.17 = (bf16[2,256,896]{2,1,0:T(8,128)(2,1)}, bf16[2,256,896]{2,1,0:T(8,128)(2,1)}, u32[]{:S(2)}, u32[]{:S(2)}) collective-permute-start(bf16[2,256,896]{2,1,0:T(8,128)(2,1)} %collective-permute-done.16), channel_id=1, source_target_pairs={{4,0},{8,4},{12,8},{16,12},{20,16},{24,20},{28,24},{32,28},{36,32}... | collective-permute-start | bytes 2752520 | tf_op jit(solution)/shard_map/ppermute | solution.py:16
  299.2 8.4 %copy.89 = f32[16,64,14,64]{1,0,3,2:T(8,128)} copy(f32[16,64,14,64]{1,3,2,0:T(8,128)S(1)} %select_bitcast_fusion) | data formatting | bytes 7340032 | tf_op jit(solution)/shard_map/transpose | solution.py:196
  307.6 7.3 %reshape.575 = f32[1024,896]{0,1:T(8,128)} reshape(f32[16,64,14,64]{1,0,3,2:T(8,128)} %copy.89) | data formatting | bytes 7340032 | tf_op jit(solution)/shard_map/reshape | solution.py:196
  318.9 10.5 %psum.7 = f32[256]{0:T(256)S(1)} all-reduce(f32[256]{0:T(256)S(1)} %multiply_reduce_fusion), channel_id=1, replica_groups=mesh['seq'=32,'tp'=4] {'tp'}, use_global_device_ids=true, to_apply=%region_6.7 | all-reduce | flops 256 | bytes 2048 | tf_op jit(solution)/shard_map/psum | solution.py:208
  329.6 6.9 %fusion.151 = f32[256,3584]{1,0:T(8,128)} fusion(bf16[256,896]{0,1:T(8,128)(2,1)S(1)} %multiply_convert_fusion, bf16[896,3584]{1,0:T(8,128)(2,1)} %param.40), kind=kOutput, calls=%fused_computation.376 | convolution fusion | flops 1644167168 | bytes 10551296 | tf_op jit(solution)/shard_map/dot_general | solution.py:215
  407.5 6.4 %fusion.152 = f32[256,896]{1,0:T(8,128)} fusion(bf16[256,3584]{1,0:T(8,128)(2,1)} %all-gather.2.cloned.1.call-done, bf16[3584,896]{1,0:T(8,128)(2,1)} %param.42), kind=kOutput, calls=%fused_computation.377 | convolution fusion | flops 1644167168 | bytes 9175040 | tf_op jit(solution)/shard_map/dot_general | solution.py:228
  416.5 56.6 %while.2 = (s32[]{:T(128)}, bf16[4,256,224]{1,2,0:T(8,128)(2,1)}, s32[4]{0:T(128)S(1)}, bf16[256,896]{1,0:T(8,128)(2,1)S(1)}, bf16[7424,896]{1,0:T(8,128)(2,1)},...) while((s32[]{:T(128)}, bf16[4,256,224]{1,2,0:T(8,128)(2,1)}, ...), condition=%wide.region_30.31_spmd, body=%wide.region_27.30_spmd.sunk | while | flops 1718148608 | bytes 32561836 | solution.py:281
  418.0 5.4 %fusion.168 = (f32[256]{0:T(256)S(1)}, f32[256,7424]{1,0:T(8,128)S(1)}) fusion(pred[256,7424]{1,0:T(32,128)(4,1)S(1)} %get-tuple-element.338, bf16[7424,896]{1,0:T(8,128)(2,1)} %get-tuple-element.337, s32[]{:T(128)S(6)} %select_n.229, bf16[256,896]{1,0:T(8,128)(2,1)S(1)} %get-tuple-element.336), kind=kOutput, calls=%fused_computation.374.clone.1 | convolution fusion | flops 857145088 | bytes 13436928 | tf_op jit(solution)/shard_map/while/body/eval_jaxpr/dot_general | solution.py:270
  424.6 6.6 %fusion.170 = bf16[4,256,224]{1,2,0:T(8,128)(2,1)} fusion(bf16[4,256,224]{1,2,0:T(8,128)(2,1)} %get-tuple-element.323, s32[]{:T(128)} %get-tuple-element.322, bf16[7424,896]{1,0:T(8,128)(2,1)} %get-tuple-element.339, s32[]{:T(128)S(6)} %select_n.229, f32[256,7424]{1,0:T(8,128)S(1)} %get-tuple-element.309, f32[256]{0:T(256)S(1)} %fusion.169, ...), kind=kOutput, calls=%fused_computation.11.clone.1 | convolution fusion | flops 857202688 | bytes 11520516 | tf_op jit(solution)/shard_map/while/body/eval_jaxpr/dot_general | solution.py:279
  432.4 5.3 %fusion.168 = (f32[256]{0:T(256)S(1)}, f32[256,7424]{1,0:T(8,128)S(1)}) fusion(pred[256,7424]{1,0:T(32,128)(4,1)S(1)} %get-tuple-element.338, bf16[7424,896]{1,0:T(8,128)(2,1)} %get-tuple-element.337, s32[]{:T(128)S(6)} %select_n.229, bf16[256,896]{1,0:T(8,128)(2,1)S(1)} %get-tuple-element.336), kind=kOutput, calls=%fused_computation.374.clone.1 | convolution fusion | flops 857145088 | bytes 13436928 | tf_op jit(solution)/shard_map/while/body/eval_jaxpr/dot_general | solution.py:270
  439.0 6.6 %fusion.170 = bf16[4,256,224]{1,2,0:T(8,128)(2,1)} fusion(bf16[4,256,224]{1,2,0:T(8,128)(2,1)} %get-tuple-element.323, s32[]{:T(128)} %get-tuple-element.322, bf16[7424,896]{1,0:T(8,128)(2,1)} %get-tuple-element.339, s32[]{:T(128)S(6)} %select_n.229, f32[256,7424]{1,0:T(8,128)S(1)} %get-tuple-element.309, f32[256]{0:T(256)S(1)} %fusion.169, ...), kind=kOutput, calls=%fused_computation.11.clone.1 | convolution fusion | flops 857202688 | bytes 11520516 | tf_op jit(solution)/shard_map/while/body/eval_jaxpr/dot_general | solution.py:279
  446.8 5.3 %fusion.168 = (f32[256]{0:T(256)S(1)}, f32[256,7424]{1,0:T(8,128)S(1)}) fusion(pred[256,7424]{1,0:T(32,128)(4,1)S(1)} %get-tuple-element.338, bf16[7424,896]{1,0:T(8,128)(2,1)} %get-tuple-element.337, s32[]{:T(128)S(6)} %select_n.229, bf16[256,896]{1,0:T(8,128)(2,1)S(1)} %get-tuple-element.336), kind=kOutput, calls=%fused_computation.374.clone.1 | convolution fusion | flops 857145088 | bytes 13436928 | tf_op jit(solution)/shard_map/while/body/eval_jaxpr/dot_general | solution.py:270
  453.3 6.6 %fusion.170 = bf16[4,256,224]{1,2,0:T(8,128)(2,1)} fusion(bf16[4,256,224]{1,2,0:T(8,128)(2,1)} %get-tuple-element.323, s32[]{:T(128)} %get-tuple-element.322, bf16[7424,896]{1,0:T(8,128)(2,1)} %get-tuple-element.339, s32[]{:T(128)S(6)} %select_n.229, f32[256,7424]{1,0:T(8,128)S(1)} %get-tuple-element.309, f32[256]{0:T(256)S(1)} %fusion.169, ...), kind=kOutput, calls=%fused_computation.11.clone.1 | convolution fusion | flops 857202688 | bytes 11520516 | tf_op jit(solution)/shard_map/while/body/eval_jaxpr/dot_general | solution.py:279
  467.1 6.1 %fusion.170 = bf16[4,256,224]{1,2,0:T(8,128)(2,1)} fusion(bf16[4,256,224]{1,2,0:T(8,128)(2,1)} %get-tuple-element.323, s32[]{:T(128)} %get-tuple-element.322, bf16[7424,896]{1,0:T(8,128)(2,1)} %get-tuple-element.339, s32[]{:T(128)S(6)} %select_n.229, f32[256,7424]{1,0:T(8,128)S(1)} %get-tuple-element.309, f32[256]{0:T(256)S(1)} %fusion.169, ...), kind=kOutput, calls=%fused_computation.11.clone.1 | convolution fusion | flops 857202688 | bytes 11520516 | tf_op jit(solution)/shard_map/while/body/eval_jaxpr/dot_general | solution.py:279
  (261 shorter events, 183.0 us)
Async XLA Ops:
  7.2 406.7 %copy-start = (bf16[3584,128]{1,0:T(8,128)(2,1)S(1)}, bf16[3584,128]{1,0:T(8,128)(2,1)}, u32[]{:S(2)}) copy-start(bf16[3584,128]{1,0:T(8,128)(2,1)} %param.43) | copy-start | bytes 2752516
  7.2 175.6 %copy-start.16 = (bf16[256,128]{1,0:T(8,128)(2,1)S(1)}, bf16[256,128]{1,0:T(8,128)(2,1)}, u32[]{:S(2)}) copy-start(bf16[256,128]{1,0:T(8,128)(2,1)} %param.29) | copy-start | bytes 196612
  7.2 371.1 %reduce-scatter.2.cloned.1.call-start = ((), (), s32[]{:S(2)}) async-start(), calls=%async_computation.1 | async-start | bytes 4587520 | tf_op jit(solution)/shard_map/reduce_scatter | solution.py:214
  9.1 26.8 %collective-permute-start = (bf16[4,256,896]{2,1,0:T(8,128)(2,1)S(1)}, bf16[4,256,896]{2,1,0:T(8,128)(2,1)}, u32[]{:S(2)}, u32[]{:S(2)}) collective-permute-start(bf16[4,256,896]{2,1,0:T(8,128)(2,1)S(1)} %pad_maximum_fusion), channel_id=1, source_target_pairs={{0,4},{4,8},{8,12},{12,16},{16,20},{20,24},{24,28},{28,32},{32,36}... | collective-permute-start | bytes 5505032 | tf_op jit(solution)/shard_map/ppermute | solution.py:16
  13.2 107.0 %collective-permute-start.9 = (bf16[2,256,896]{2,1,0:T(8,128)(2,1)}, bf16[2,256,896]{2,1,0:T(8,128)(2,1)}, u32[]{:S(2)}, u32[]{:S(2)}) collective-permute-start(bf16[2,256,896]{2,1,0:T(8,128)(2,1)} %pad_maximum_fusion.1), channel_id=1, source_target_pairs={{4,0},{8,4},{12,8},{16,12},{20,16},{24,20},{28,24},{32,28},{36,32}... | collective-permute-start | bytes 2752520 | tf_op jit(solution)/shard_map/ppermute | solution.py:16
  19.7 174.8 %collective-permute-start.18 = (bf16[3,896]{1,0:T(4,128)(2,1)S(1)}, bf16[3,896]{1,0:T(4,128)(2,1)S(1)}, u32[]{:S(2)}, u32[]{:S(2)}) collective-permute-start(bf16[3,896]{1,0:T(4,128)(2,1)S(1)} %slice.293), channel_id=1, source_target_pairs={{0,4},{4,8},{8,12},{12,16},{16,20},{20,24},{24,28},{28,32},{32,36}... | collective-permute-start | bytes 16136 | tf_op jit(solution)/shard_map/ppermute | solution.py:16
  22.3 160.5 %collective-permute-start.19 = (bf16[3,128]{1,0:T(4,128)(2,1)S(1)}, bf16[3,128]{1,0:T(4,128)(2,1)S(1)}, u32[]{:S(2)}, u32[]{:S(2)}) collective-permute-start(bf16[3,128]{1,0:T(4,128)(2,1)S(1)} %slice.304), channel_id=1, source_target_pairs={{0,4},{4,8},{8,12},{12,16},{16,20},{20,24},{24,28},{28,32},{32,36}... | collective-permute-start | bytes 2312 | tf_op jit(solution)/shard_map/ppermute | solution.py:16
  35.8 27.0 %collective-permute-start.1 = (bf16[4,256,896]{2,1,0:T(8,128)(2,1)}, bf16[4,256,896]{2,1,0:T(8,128)(2,1)}, u32[]{:S(2)}, u32[]{:S(2)}) collective-permute-start(bf16[4,256,896]{2,1,0:T(8,128)(2,1)} %collective-permute-done), channel_id=1, source_target_pairs={{0,4},{4,8},{8,12},{12,16},{16,20},{20,24},{24,28},{28,32},{32,36}... | collective-permute-start | bytes 5505032 | tf_op jit(solution)/shard_map/ppermute | solution.py:16
  62.8 26.9 %collective-permute-start.2 = (bf16[4,256,896]{2,1,0:T(8,128)(2,1)}, bf16[4,256,896]{2,1,0:T(8,128)(2,1)S(1)}, u32[]{:S(2)}, u32[]{:S(2)}) collective-permute-start(bf16[4,256,896]{2,1,0:T(8,128)(2,1)} %collective-permute-done.1), channel_id=1, source_target_pairs={{0,4},{4,8},{8,12},{12,16},{16,20},{20,24},{24,28},{28,32},{32,36}... | collective-permute-start | bytes 5505032 | tf_op jit(solution)/shard_map/ppermute | solution.py:16
  89.7 26.7 %collective-permute-start.3 = (bf16[4,256,896]{2,1,0:T(8,128)(2,1)S(1)}, bf16[4,256,896]{2,1,0:T(8,128)(2,1)}, u32[]{:S(2)}, u32[]{:S(2)}) collective-permute-start(bf16[4,256,896]{2,1,0:T(8,128)(2,1)S(1)} %collective-permute-done.2), channel_id=1, source_target_pairs={{0,4},{4,8},{8,12},{12,16},{16,20},{20,24},{24,28},{28,32},{32,36}... | collective-permute-start | bytes 5505032 | tf_op jit(solution)/shard_map/ppermute | solution.py:16
  116.4 27.9 %collective-permute-start.4 = (bf16[4,256,896]{2,1,0:T(8,128)(2,1)}, bf16[4,256,896]{2,1,0:T(8,128)(2,1)}, u32[]{:S(2)}, u32[]{:S(2)}) collective-permute-start(bf16[4,256,896]{2,1,0:T(8,128)(2,1)} %collective-permute-done.3), channel_id=1, source_target_pairs={{0,4},{4,8},{8,12},{12,16},{16,20},{20,24},{24,28},{28,32},{32,36}... | collective-permute-start | bytes 5505032 | tf_op jit(solution)/shard_map/ppermute | solution.py:16
  120.2 17.0 %collective-permute-start.10 = (bf16[2,256,896]{2,1,0:T(8,128)(2,1)}, bf16[2,256,896]{2,1,0:T(8,128)(2,1)}, u32[]{:S(2)}, u32[]{:S(2)}) collective-permute-start(bf16[2,256,896]{2,1,0:T(8,128)(2,1)} %collective-permute-done.9), channel_id=1, source_target_pairs={{4,0},{8,4},{12,8},{16,12},{20,16},{24,20},{28,24},{32,28},{36,32}... | collective-permute-start | bytes 2752520 | tf_op jit(solution)/shard_map/ppermute | solution.py:16
  137.2 17.1 %collective-permute-start.11 = (bf16[2,256,896]{2,1,0:T(8,128)(2,1)}, bf16[2,256,896]{2,1,0:T(8,128)(2,1)}, u32[]{:S(2)}, u32[]{:S(2)}) collective-permute-start(bf16[2,256,896]{2,1,0:T(8,128)(2,1)} %collective-permute-done.10), channel_id=1, source_target_pairs={{4,0},{8,4},{12,8},{16,12},{20,16},{24,20},{28,24},{32,28},{36,32}... | collective-permute-start | bytes 2752520 | tf_op jit(solution)/shard_map/ppermute | solution.py:16
  144.4 33.2 %collective-permute-start.5 = (bf16[4,256,896]{2,1,0:T(8,128)(2,1)}, bf16[4,256,896]{2,1,0:T(8,128)(2,1)}, u32[]{:S(2)}, u32[]{:S(2)}) collective-permute-start(bf16[4,256,896]{2,1,0:T(8,128)(2,1)} %collective-permute-done.4), channel_id=1, source_target_pairs={{0,4},{4,8},{8,12},{12,16},{16,20},{20,24},{24,28},{28,32},{32,36}... | collective-permute-start | bytes 5505032 | tf_op jit(solution)/shard_map/ppermute | solution.py:16
  154.3 17.1 %collective-permute-start.12 = (bf16[2,256,896]{2,1,0:T(8,128)(2,1)}, bf16[2,256,896]{2,1,0:T(8,128)(2,1)}, u32[]{:S(2)}, u32[]{:S(2)}) collective-permute-start(bf16[2,256,896]{2,1,0:T(8,128)(2,1)} %collective-permute-done.11), channel_id=1, source_target_pairs={{4,0},{8,4},{12,8},{16,12},{20,16},{24,20},{28,24},{32,28},{36,32}... | collective-permute-start | bytes 2752520 | tf_op jit(solution)/shard_map/ppermute | solution.py:16
  171.4 17.1 %collective-permute-start.13 = (bf16[2,256,896]{2,1,0:T(8,128)(2,1)}, bf16[2,256,896]{2,1,0:T(8,128)(2,1)}, u32[]{:S(2)}, u32[]{:S(2)}) collective-permute-start(bf16[2,256,896]{2,1,0:T(8,128)(2,1)} %collective-permute-done.12), channel_id=1, source_target_pairs={{4,0},{8,4},{12,8},{16,12},{20,16},{24,20},{28,24},{32,28},{36,32}... | collective-permute-start | bytes 2752520 | tf_op jit(solution)/shard_map/ppermute | solution.py:16
  177.6 38.3 %collective-permute-start.6 = (bf16[4,256,896]{2,1,0:T(8,128)(2,1)}, bf16[4,256,896]{2,1,0:T(8,128)(2,1)}, u32[]{:S(2)}, u32[]{:S(2)}) collective-permute-start(bf16[4,256,896]{2,1,0:T(8,128)(2,1)} %collective-permute-done.5), channel_id=1, source_target_pairs={{0,4},{4,8},{8,12},{12,16},{16,20},{20,24},{24,28},{28,32},{32,36}... | collective-permute-start | bytes 5505032 | tf_op jit(solution)/shard_map/ppermute | solution.py:16
  188.6 25.4 %collective-permute-start.14 = (bf16[2,256,896]{2,1,0:T(8,128)(2,1)}, bf16[2,256,896]{2,1,0:T(8,128)(2,1)}, u32[]{:S(2)}, u32[]{:S(2)}) collective-permute-start(bf16[2,256,896]{2,1,0:T(8,128)(2,1)} %collective-permute-done.13), channel_id=1, source_target_pairs={{4,0},{8,4},{12,8},{16,12},{20,16},{24,20},{28,24},{32,28},{36,32}... | collective-permute-start | bytes 2752520 | tf_op jit(solution)/shard_map/ppermute | solution.py:16
  202.0 16.3 %collective-permute-start.21 = (f32[14,64,64]{2,1,0:T(8,128)S(1)}, f32[14,64,64]{2,1,0:T(8,128)S(1)}, u32[]{:S(2)}, u32[]{:S(2)}) collective-permute-start(f32[14,64,64]{2,1,0:T(8,128)S(1)} %convolution_add_fusion.1), channel_id=1, source_target_pairs={{0,4},{4,8},{8,12},{12,16},{16,20},{20,24},{24,28},{28,32},{32,36}... | collective-permute-start | bytes 688136 | tf_op jit(solution)/shard_map/ppermute | solution.py:16
  205.2 8.7 %collective-permute-start.20 = (f32[14]{0:T(128)S(1)}, f32[14]{0:T(128)S(1)}, u32[]{:S(2)}, u32[]{:S(2)}) collective-permute-start(f32[14]{0:T(128)S(1)} %get-tuple-element.79), channel_id=1, source_target_pairs={{0,4},{4,8},{8,12},{12,16},{16,20},{20,24},{24,28},{28,32},{32,36}... | collective-permute-start | bytes 176 | tf_op jit(solution)/shard_map/ppermute | solution.py:16
  214.0 31.5 %collective-permute-start.15 = (bf16[2,256,896]{2,1,0:T(8,128)(2,1)}, bf16[2,256,896]{2,1,0:T(8,128)(2,1)}, u32[]{:S(2)}, u32[]{:S(2)}) collective-permute-start(bf16[2,256,896]{2,1,0:T(8,128)(2,1)} %collective-permute-done.14), channel_id=1, source_target_pairs={{4,0},{8,4},{12,8},{16,12},{20,16},{24,20},{28,24},{32,28},{36,32}... | collective-permute-start | bytes 2752520 | tf_op jit(solution)/shard_map/ppermute | solution.py:16
  215.9 70.4 %collective-permute-start.7 = (bf16[4,256,896]{2,1,0:T(8,128)(2,1)}, bf16[4,256,896]{2,1,0:T(8,128)(2,1)}, u32[]{:S(2)}, u32[]{:S(2)}) collective-permute-start(bf16[4,256,896]{2,1,0:T(8,128)(2,1)} %collective-permute-done.6), channel_id=1, source_target_pairs={{0,4},{4,8},{8,12},{12,16},{16,20},{20,24},{24,28},{28,32},{32,36}... | collective-permute-start | bytes 5505032 | tf_op jit(solution)/shard_map/ppermute | solution.py:16
  218.5 17.6 %collective-permute-start.23 = (f32[14,64,64]{2,1,0:T(8,128)S(1)}, f32[14,64,64]{2,1,0:T(8,128)}, u32[]{:S(2)}, u32[]{:S(2)}) collective-permute-start(f32[14,64,64]{2,1,0:T(8,128)S(1)} %multiply_add_fusion.3), channel_id=1, source_target_pairs={{0,8},{4,12},{8,16},{12,20},{16,24},{20,28},{24,32},{28,36},{32,40... | collective-permute-start | bytes 688136 | tf_op jit(solution)/shard_map/ppermute | solution.py:16
  223.2 12.8 %collective-permute-start.22 = (f32[14]{0:T(128)S(1)}, f32[14]{0:T(128)S(1)}, u32[]{:S(2)}, u32[]{:S(2)}) collective-permute-start(f32[14]{0:T(128)S(1)} %mul.384), channel_id=1, source_target_pairs={{0,8},{4,12},{8,16},{12,20},{16,24},{20,28},{24,32},{28,36},{32,40... | collective-permute-start | bytes 176 | tf_op jit(solution)/shard_map/ppermute | solution.py:16
  237.2 31.9 %collective-permute-start.25 = (f32[14,64,64]{2,1,0:T(8,128)S(1)}, f32[14,64,64]{2,1,0:T(8,128)S(1)}, u32[]{:S(2)}, u32[]{:S(2)}) collective-permute-start(f32[14,64,64]{2,1,0:T(8,128)S(1)} %multiply_add_fusion.2), channel_id=1, source_target_pairs={{0,16},{4,20},{8,24},{12,28},{16,32},{20,36},{24,40},{28,44},{32,4... | collective-permute-start | bytes 688136 | tf_op jit(solution)/shard_map/ppermute | solution.py:16
  239.3 29.7 %collective-permute-start.24 = (f32[14]{0:T(128)S(1)}, f32[14]{0:T(128)S(1)}, u32[]{:S(2)}, u32[]{:S(2)}) collective-permute-start(f32[14]{0:T(128)S(1)} %mul.387), channel_id=1, source_target_pairs={{0,16},{4,20},{8,24},{12,28},{16,32},{20,36},{24,40},{28,44},{32,4... | collective-permute-start | bytes 176 | tf_op jit(solution)/shard_map/ppermute | solution.py:16
  245.5 43.7 %collective-permute-start.16 = (bf16[2,256,896]{2,1,0:T(8,128)(2,1)}, bf16[2,256,896]{2,1,0:T(8,128)(2,1)}, u32[]{:S(2)}, u32[]{:S(2)}) collective-permute-start(bf16[2,256,896]{2,1,0:T(8,128)(2,1)} %collective-permute-done.15), channel_id=1, source_target_pairs={{4,0},{8,4},{12,8},{16,12},{20,16},{24,20},{28,24},{32,28},{36,32}... | collective-permute-start | bytes 2752520 | tf_op jit(solution)/shard_map/ppermute | solution.py:16
  269.2 13.5 %collective-permute-start.26 = (f32[14,64,64]{2,1,0:T(8,128)S(1)}, f32[14,64,64]{2,1,0:T(8,128)S(1)}, u32[]{:S(2)}, u32[]{:S(2)}) collective-permute-start(f32[14,64,64]{2,1,0:T(8,128)S(1)} %multiply_add_fusion.1), channel_id=1, source_target_pairs={{0,32},{4,36},{8,40},{12,44},{16,48},{20,52},{24,56},{28,60},{32,6... | collective-permute-start | bytes 688136 | tf_op jit(solution)/shard_map/ppermute | solution.py:16
  282.8 12.3 %collective-permute-start.27 = (f32[14,64,64]{2,1,0:T(8,128)S(1)}, f32[14,64,64]{2,1,0:T(8,128)S(1)}, u32[]{:S(2)}, u32[]{:S(2)}) collective-permute-start(f32[14,64,64]{2,1,0:T(8,128)S(1)} %multiply_add_fusion), channel_id=1, source_target_pairs={{0,4},{4,8},{8,12},{12,16},{16,20},{20,24},{24,28},{28,32},{32,36}... | collective-permute-start | bytes 688136 | tf_op jit(solution)/shard_map/ppermute | solution.py:16
  286.3 43.2 %collective-permute-start.8 = (bf16[4,256,896]{2,1,0:T(8,128)(2,1)}, bf16[4,256,896]{2,1,0:T(8,128)(2,1)}, u32[]{:S(2)}, u32[]{:S(2)}) collective-permute-start(bf16[4,256,896]{2,1,0:T(8,128)(2,1)} %collective-permute-done.7), channel_id=1, source_target_pairs={{0,4},{4,8},{8,12},{12,16},{16,20},{20,24},{24,28},{28,32},{32,36}... | collective-permute-start | bytes 5505032 | tf_op jit(solution)/shard_map/ppermute | solution.py:16
  289.2 40.4 %collective-permute-start.17 = (bf16[2,256,896]{2,1,0:T(8,128)(2,1)}, bf16[2,256,896]{2,1,0:T(8,128)(2,1)}, u32[]{:S(2)}, u32[]{:S(2)}) collective-permute-start(bf16[2,256,896]{2,1,0:T(8,128)(2,1)} %collective-permute-done.16), channel_id=1, source_target_pairs={{4,0},{8,4},{12,8},{16,12},{20,16},{24,20},{28,24},{32,28},{36,32}... | collective-permute-start | bytes 2752520 | tf_op jit(solution)/shard_map/ppermute | solution.py:16
  336.5 71.0 %all-gather.2.cloned.1.call-start = ((), (), s32[]{:S(2)}) async-start(), calls=%async_computation.2 | async-start | bytes 2293760 | tf_op jit(solution)/shard_map/all_gather | solution.py:225
  (15 other events, 805.8 us)
Sparse Core Ops, SparseCore 0:
  336.6 39.0 reduce-scatter.1
  381.7 25.7 all-gather.1
